TPU v7x, 32 devices: a whole 2x2x4 slice. The times are simulated.
32 devices in a mesh: phase: 4 (over y, x), rows: 8 (over z, core).
Axes of the slice: x: 2, y: 2, z: 4, core: 2. Of those that a mesh axis runs over, the one named last changes fastest.
Arguments:
- frames: bfloat16 [2, 192, 16, 128], P(None, None, 'rows'), may hold values from -12 to 12, as said below
- causal_cache: bfloat16 [4, 2, 2, 192, 16, 128], P('phase', None, None, None, 'rows'), may hold values from -4 to 4
- conv_weight: bfloat16 [4, 2, 3, 3, 3, 192, 192], P('phase'), may hold values from -0.15625 to 0.15625
- conv_bias: float32 [4, 2, 192], P('phase'), may hold values from -3 to 3
- norm_gain: float32 [4, 2, 192], P('phase'), may hold values from 0.1 to 1.9
- norm_shift: float32 [4, 2, 192], P('phase'), may hold values from -3 to 3
Outputs:
- phase_out: bfloat16 [4, 2, 192, 16, 128], P('phase', None, None, 'rows')
- new_cache: bfloat16 [4, 2, 2, 192, 16, 128], P('phase', None, None, None, 'rows')
Inputs may be any that keep to these rules, and one draw needn't show every extreme that they name: `frames`: Real-valued frame features.
All inputs are finite; a program needn't handle non-finite values.
Results may differ from a plain program's by a relative error of at most 0.0066.
Values may be sent and summed in bfloat16 or wider, within the bound.
No kernel may reach another device: no remote copies, remote signals or barrier semaphores. Data moves between devices by JAX's collectives and lax.ppermute only.
A program may use at most 64 MiB of HBM per device.

v0:
```python
import jax
import jax.numpy as jnp
from jax import lax
from jax.sharding import PartitionSpec as P
from jax.experimental import pallas as pl
from jax.experimental.pallas import tpu as pltpu
import functools

GROUPS = 32
EPS = 1e-06
MAX_SPAN = 16


def span_devices(peers, rows_here):
    count = 1
    while count * 2 <= peers and peers % (count * 2) == 0 and count * 2 * rows_here <= MAX_SPAN:
        count *= 2
    return count


def gather_span(array, dim, span_count):
    if span_count == 1:
        return array
    peers = lax.axis_size("rows")
    if span_count == peers:
        return lax.all_gather(array, "rows", axis=dim, tiled=True)
    place = lax.axis_index("rows") % span_count
    pieces = [array]
    for shift in range(1, span_count):
        pairs = [
            (b * span_count + p, b * span_count + (p + shift) % span_count)
            for b in range(peers // span_count)
            for p in range(span_count)
        ]
        pieces.append(lax.ppermute(array, "rows", pairs))
    stacked = jnp.stack(pieces)
    order = (place - jnp.arange(span_count)) % span_count
    picked = jnp.take(stacked, order, axis=0)
    picked = jnp.moveaxis(picked, 0, dim)
    shape = list(array.shape)
    shape[dim] = shape[dim] * span_count
    return picked.reshape(shape)


def with_rim(array, dim, span_count):
    peers = lax.axis_size("rows")
    length = array.shape[dim]
    if span_count == peers:
        return array
    up = [(i, i + span_count) for i in range(peers - span_count)]
    down = [(j, i) for i, j in up]
    last = lax.slice_in_dim(array, length - 1, length, axis=dim)
    leading = lax.slice_in_dim(array, 0, 1, axis=dim)
    before = lax.ppermute(last, "rows", up)
    after = lax.ppermute(leading, "rows", down)
    return jnp.concatenate([before, array, after], axis=dim)


def pass_on(result, span_count):
    phase_count = lax.axis_size("phase")
    forward = [(s, s + 1) for s in range(phase_count - 1)]
    length = result.shape[0]
    if span_count % 2 or length % 2:
        return lax.ppermute(result, "phase", forward)
    peers = lax.axis_size("rows")
    half = length // 2
    core = lax.axis_index("rows") % 2
    mine = lax.dynamic_slice_in_dim(result, core * half, half, axis=0)
    got = lax.ppermute(mine, "phase", forward)
    other = lax.ppermute(got, "rows", [(i, i ^ 1) for i in range(peers)])
    return jnp.where(core == 0, jnp.concatenate([got, other]), jnp.concatenate([other, got]))


def arrange_taps(weight):
    outputs = weight.shape[3]
    channels = weight.shape[4]
    return jnp.transpose(weight, (2, 3, 0, 1, 4)).reshape(3 * outputs, 9 * channels)


def conv_rows(x0, x1, x2, taps, bias, res, out, rows_out, padded):
    outputs = out.shape[1]
    channels = x0.shape[1]
    columns = x0.shape[2]
    pair = 4 if rows_out % 4 == 0 else (2 if rows_out % 2 == 0 else 1)
    lanes = pair * columns
    lane = lax.broadcasted_iota(jnp.int32, (outputs, lanes), 1) % columns
    frames = (x0, x1, x2)

    def column(r):
        if padded or 0 < r < rows_out - 1:
            base = r if padded else r - 1
            parts = [x[pl.ds(base, 3)] for x in frames]
            return jnp.concatenate(parts, axis=0).reshape(9 * channels, columns)
        zero = jnp.zeros((1, channels, columns), x0.dtype)
        parts = []
        for x in frames:
            for dy in range(3):
                q = r + dy - 1
                parts.append(zero if q < 0 or q >= rows_out else x[pl.ds(q, 1)])
        return jnp.concatenate(parts, axis=0).reshape(9 * channels, columns)

    for r in range(0, rows_out, pair):
        cols = [column(r + k) for k in range(pair)]
        rhs = cols[0] if pair == 1 else jnp.concatenate(cols, axis=1)
        acc = jnp.dot(taps[...], rhs, preferred_element_type=jnp.float32)
        left = pltpu.roll(acc[:outputs], 1, 1)
        right = pltpu.roll(acc[2 * outputs :], lanes - 1, 1)
        total = acc[outputs : 2 * outputs] + jnp.where(lane == 0, 0.0, left)
        total = total + jnp.where(lane == columns - 1, 0.0, right) + bias[...]
        for k in range(pair):
            piece = total[:, k * columns : (k + 1) * columns]
            if res is not None:
                piece = piece + res[r + k].astype(jnp.float32)
            out[r + k] = piece.astype(out.dtype)


def conv_body(x0, x1, x2, taps, bias, *rest, rows_out, with_res, padded):
    res = rest[0] if with_res else None
    conv_rows(x0, x1, x2, taps, bias, res, rest[-1], rows_out, padded)


def causal_conv(x0, x1, x2, taps, bias_vec, res, padded):
    rows_out = x0.shape[0] - 2 if padded else x0.shape[0]
    outputs = taps.shape[0] // 3
    args = [x0, x1, x2, taps, bias_vec.reshape(outputs, 1)]
    if res is not None:
        args.append(res)
    body = functools.partial(conv_body, rows_out=rows_out, with_res=res is not None, padded=padded)
    shape = jax.ShapeDtypeStruct((rows_out, outputs, x0.shape[2]), jnp.bfloat16)
    return pl.pallas_call(body, out_shape=shape)(*args)


def conv_span(x0, x1, x2, taps, bias, res, out, base, count):
    outputs = out.shape[1]
    channels = x0.shape[1]
    columns = x0.shape[2]
    pair = 4 if count % 4 == 0 else (2 if count % 2 == 0 else 1)
    lanes = pair * columns
    lane = lax.broadcasted_iota(jnp.int32, (outputs, lanes), 1) % columns

    def step(i, carry):
        r = base + i * pair
        cols = []
        for k in range(pair):
            parts = [x[pl.ds(r + k, 3)] for x in (x0, x1, x2)]
            cols.append(jnp.concatenate(parts, axis=0).reshape(9 * channels, columns))
        rhs = cols[0] if pair == 1 else jnp.concatenate(cols, axis=1)
        acc = jnp.dot(taps[...], rhs, preferred_element_type=jnp.float32)
        left = pltpu.roll(acc[:outputs], 1, 1)
        right = pltpu.roll(acc[2 * outputs :], lanes - 1, 1)
        total = acc[outputs : 2 * outputs] + jnp.where(lane == 0, 0.0, left)
        total = total + jnp.where(lane == columns - 1, 0.0, right) + bias[...]
        for k in range(pair):
            piece = total[:, k * columns : (k + 1) * columns]
            if res is not None:
                piece = piece + res[r + k].astype(jnp.float32)
            out[i * pair + k] = piece.astype(out.dtype)
        return carry

    lax.fori_loop(0, count // pair, step, 0)


def fused_body(flags, caches, a_p, a_pp, frames, src_b, src_c, taps, bias, member, gain, shift, *rest, kind):
    rest = list(rest)
    own = rest.pop(0) if kind != "first" else None
    if kind == "tail":
        out, x0, x1, rawbuf, sems = rest
        act = own
    else:
        out, act, x0, x1, rawbuf, sems = rest
    span, channels, columns = rawbuf.shape
    half = span // 2
    first, second, mode, core = flags[0], flags[1], flags[2], flags[6]
    c0, c1 = caches.at[flags[4]], caches.at[flags[5]]
    whole = frames.at[flags[3]]
    top, bottom = rawbuf.at[pl.ds(0, half)], rawbuf.at[pl.ds(half, half)]
    inner0, inner1 = x0.at[pl.ds(1, span)], x1.at[pl.ds(1, span)]

    def inner(x):
        return x.at[pl.ds(1, span)]

    def begin(pairs, base):
        for i, (a, b) in enumerate(pairs):
            pltpu.make_async_copy(a, b, sems.at[base + i]).start()

    def finish(pairs, base):
        for i, (a, b) in enumerate(pairs):
            pltpu.make_async_copy(a, b, sems.at[base + i]).wait()

    @pl.when(mode == 0)
    def _():
        begin([(whole.at[pl.ds(0, half)], top), (whole.at[pl.ds(half, half)], bottom)], 0)

    @pl.when(mode == 1)
    def _():
        begin([(src_b, top), (src_c, bottom)], 0)

    @pl.when(mode == 2)
    def _():
        begin([(src_c, top), (src_b, bottom)], 0)

    @pl.when(first == 1)
    def _():
        begin([(c0, inner0), (c1, inner1)], 2)

    @pl.when(jnp.logical_and(first == 0, second == 1))
    def _():
        begin([(c1, inner0), (inner(a_p), inner1)], 2)

    @pl.when(jnp.logical_and(first == 0, second == 0))
    def _():
        begin([(inner(a_pp), inner0), (inner(a_p), inner1)], 2)

    zero = jnp.zeros((channels, columns), x0.dtype)
    for x in (x0, x1):
        x[0] = zero
        x[span + 1] = zero
    source_copies = [(src_b, top), (src_c, bottom)]
    history_copies = [(inner(a_pp), inner0), (inner(a_p), inner1)]

    if kind != "tail":
        if kind == "first":
            finish(source_copies, 0)
            raw = rawbuf
        else:
            raw = own
        count = float(span * columns * (channels // GROUPS))

        def group_total(acc):
            spread = jnp.dot(member[...], acc, precision=lax.Precision.HIGHEST, preferred_element_type=jnp.float32)
            return jnp.sum(spread, axis=1, keepdims=True)

        acc = raw[0].astype(jnp.float32)
        for r in range(1, span):
            acc = acc + raw[r].astype(jnp.float32)
        average = group_total(acc) / count
        acc = jnp.square(raw[0].astype(jnp.float32) - average)
        for r in range(1, span):
            acc = acc + jnp.square(raw[r].astype(jnp.float32) - average)
        inverse = lax.rsqrt(group_total(acc) / count + EPS)
        act[0] = zero
        act[span + 1] = zero
        for r in range(span):
            value = (raw[r].astype(jnp.float32) - average) * inverse
            value = value * gain[...] + shift[...]
            act[r + 1] = (value / (1.0 + jnp.exp(-value))).astype(act.dtype)

    finish(history_copies, 2)
    if kind == "first":
        conv_span(x0, x1, act, taps, bias, None, out, 0, span)
    else:
        finish(source_copies, 0)
        base = core * half if kind == "lead" else (1 - core) * half
        conv_span(x0, x1, act, taps, bias, rawbuf, out, base, half)


def fused_conv(flags, caches, cache_at, recent, frames, frame_at, halves, taps, bias_vec, norm, kind, own=None):
    span, channels, columns = caches.shape[1:]
    outputs = taps.shape[0] // 3
    group_of = jnp.arange(channels) // (channels // GROUPS)
    member = (group_of[:, None] == group_of[None, :]).astype(jnp.float32)
    vmem = pl.BlockSpec(memory_space=pltpu.VMEM)
    anywhere = pl.BlockSpec(memory_space=pl.ANY)
    flags = jnp.concatenate([flags[:3], jnp.array([frame_at, cache_at[0], cache_at[1]], jnp.int32), flags[3:]])
    args = [flags, caches, recent[0], recent[1], frames, halves[0], halves[1]]
    args += [taps, bias_vec.reshape(outputs, 1), member]
    args += [v.reshape(-1, 1).astype(jnp.float32) for v in norm]
    specs = [pl.BlockSpec(memory_space=pltpu.SMEM)] + [anywhere] * 6 + [vmem] * 5
    if own is not None:
        args.append(own)
        specs.append(vmem)
    rows_out = span if kind == "first" else span // 2
    result = jax.ShapeDtypeStruct((rows_out, outputs, columns), jnp.bfloat16)
    padded = jax.ShapeDtypeStruct((span + 2, channels, columns), jnp.bfloat16)
    shapes = result if kind == "tail" else (result, padded)
    body = functools.partial(fused_body, kind=kind)
    return pl.pallas_call(
        body,
        out_shape=shapes,
        in_specs=specs,
        out_specs=vmem if kind == "tail" else (vmem, vmem),
        scratch_shapes=[
            pltpu.VMEM((span + 2, channels, columns), jnp.bfloat16),
            pltpu.VMEM((span + 2, channels, columns), jnp.bfloat16),
            pltpu.VMEM((span, channels, columns), jnp.bfloat16),
            pltpu.SemaphoreType.DMA((4,)),
        ],
    )(*args)


def block_sum(values, span_count):
    peers = lax.axis_size("rows")
    if span_count == peers:
        return values
    lead = (lax.axis_index("rows") % span_count == 0).astype(values.dtype)
    return lax.psum(values * lead, "rows")


def activate(source, gain_vec, shift_vec, cell_count, span_count):
    height, channels, columns = source.shape
    grouped = source.astype(jnp.float32).reshape(height, GROUPS, channels // GROUPS, columns)
    average = block_sum(jnp.sum(grouped, axis=(0, 2, 3)), span_count) / cell_count
    centred = grouped - average[None, :, None, None]
    spread = block_sum(jnp.sum(centred * centred, axis=(0, 2, 3)), span_count) / cell_count
    inverse = lax.rsqrt(spread + EPS)
    normed = (centred * inverse[None, :, None, None]).reshape(height, channels, columns)
    normed = normed * gain_vec[None, :, None] + shift_vec[None, :, None]
    return jax.nn.silu(normed).astype(jnp.bfloat16)


def run_frame(source, first_hist, second_hist, kernels, biases, gains, shifts, cell_count, span_count):
    padded = span_count != lax.axis_size("rows")
    first_in = with_rim(activate(source, gains[0], shifts[0], cell_count, span_count), 0, span_count)
    hidden = causal_conv(first_hist[0], first_hist[1], first_in, kernels[0], biases[0], None, padded)
    second_in = with_rim(activate(hidden, gains[1], shifts[1], cell_count, span_count), 0, span_count)
    result = causal_conv(second_hist[0], second_hist[1], second_in, kernels[1], biases[1], source, padded)
    return (result, (first_hist[1], first_in), (second_hist[1], second_in))


def shards_whole(frames, causal_cache, conv_weight, conv_bias, norm_gain, norm_shift):
    phase_no = lax.axis_index("phase")
    phase_count = lax.axis_size("phase")
    peers = lax.axis_size("rows")
    frame_count, channels, rows_here, columns = frames.shape
    span = rows_here * peers
    half = span // 2
    core = lax.axis_index("rows") % 2
    start = lax.axis_index("rows") * rows_here
    forward = [(s, s + 1) for s in range(phase_count - 1)]
    frames_t = jnp.transpose(frames, (0, 2, 1, 3))
    cache_t = jnp.transpose(causal_cache[0], (0, 1, 3, 2, 4))
    early = lax.all_gather(jnp.stack([frames_t[0], cache_t[0, 0], cache_t[0, 1]]), "rows", axis=1, tiled=True)
    late = lax.all_gather(
        jnp.stack([cache_t[1, 0], cache_t[1, 1]] + list(frames_t[1:])), "rows", axis=1, tiled=True
    )
    frame_of = [(early, 0)] + [(late, 2 + f) for f in range(frame_count - 1)]
    cache_of = ((early, (1, 2)), (late, (0, 1)))
    taps = (arrange_taps(conv_weight[0, 0]), arrange_taps(conv_weight[0, 1]))

    def own_rows(x, rim=0):
        return lax.dynamic_slice_in_dim(x, start + rim, rows_here, axis=0)

    got = other = jnp.zeros((half, channels, columns), jnp.bfloat16)
    acts = ([], [])
    blank = jnp.zeros((rows_here, channels, columns), jnp.bfloat16)
    blank_frame = jnp.zeros((span + 2, channels, columns), jnp.bfloat16)
    produced = [blank] * frame_count
    kept = [[blank, blank], [blank, blank]]
    mode = jnp.where(phase_no == 0, 0, 1 + core)
    tick_count = frame_count + phase_count - 1
    for tick_no in range(tick_count):
        frame_no = tick_no - phase_no
        flags = jnp.stack([frame_no == 0, frame_no == 1, mode, core]).astype(jnp.int32)
        frame_stack, frame_at = frame_of[min(tick_no, frame_count - 1)]
        recents = []
        for j in range(2):
            a_p = acts[j][-1] if acts[j] else blank_frame
            a_pp = acts[j][-2] if len(acts[j]) > 1 else blank_frame
            recents.append((a_p, a_pp))
        common = (frame_stack, frame_at, (got, other))
        hidden, first_in = fused_conv(
            flags, cache_of[0][0], cache_of[0][1], recents[0], *common,
            taps[0], conv_bias[0, 0], (norm_gain[0, 0], norm_shift[0, 0]), "first",
        )
        second = (flags, cache_of[1][0], cache_of[1][1], recents[1], *common, taps[1], conv_bias[0, 1])
        lead, second_in = fused_conv(*second, (norm_gain[0, 1], norm_shift[0, 1]), "lead", hidden)
        tail = fused_conv(*second, (norm_gain[0, 1], norm_shift[0, 1]), "tail", second_in)
        if tick_no + 1 < tick_count:
            got = lax.ppermute(lead, "phase", forward)
            got, tail = lax.optimization_barrier((got, tail))
            other = lax.ppermute(got, "rows", [(i, i ^ 1) for i in range(peers)])
        last = frame_no == frame_count - 1
        for j, a in enumerate((first_in, second_in)):
            stack, (_, k1) = cache_of[j]
            newer = jnp.where(frame_no == 0, own_rows(stack[k1]), own_rows(recents[j][0], 1))
            kept[j] = [jnp.where(last, newer, kept[j][0]), jnp.where(last, own_rows(a, 1), kept[j][1])]
            acts[j].append(a)
        mine = lax.dynamic_slice_in_dim(lead, start - core * half, rows_here, axis=0)
        theirs = lax.dynamic_slice_in_dim(tail, start - (1 - core) * half, rows_here, axis=0)
        result_rows = jnp.where(start // half == core, mine, theirs)
        for f in range(frame_count):
            if 0 <= tick_no - f < phase_count:
                produced[f] = jnp.where(frame_no == f, result_rows, produced[f])
    produced = jnp.transpose(jnp.stack(produced), (0, 2, 1, 3))
    new_cache = jnp.transpose(jnp.stack([jnp.stack(k) for k in kept]), (0, 1, 3, 2, 4))
    return (produced[None], new_cache[None])


def shards(frames, causal_cache, conv_weight, conv_bias, norm_gain, norm_shift):
    peers = lax.axis_size("rows")
    rows_here = frames.shape[2]
    if span_devices(peers, rows_here) == peers and (rows_here * peers) % 2 == 0:
        return shards_whole(frames, causal_cache, conv_weight, conv_bias, norm_gain, norm_shift)
    return shards_split(frames, causal_cache, conv_weight, conv_bias, norm_gain, norm_shift)


def shards_split(frames, causal_cache, conv_weight, conv_bias, norm_gain, norm_shift):
    phase_no = lax.axis_index("phase")
    phase_count = lax.axis_size("phase")
    peers = lax.axis_size("rows")
    frame_count = frames.shape[0]
    channels = frames.shape[1]
    rows_here = frames.shape[2]
    columns = frames.shape[3]
    span_count = span_devices(peers, rows_here)
    span = rows_here * span_count
    cell_count = float(channels // GROUPS * rows_here * peers * columns)
    padded = span_count != peers
    frames_t = jnp.transpose(frames, (0, 2, 1, 3))
    cache_t = jnp.transpose(causal_cache[0], (0, 1, 3, 2, 4))
    early = gather_span(jnp.stack([frames_t[0], cache_t[0, 0], cache_t[0, 1]]), 1, span_count)
    late = gather_span(jnp.stack([cache_t[1, 0], cache_t[1, 1]] + list(frames_t[1:])), 1, span_count)
    frames_span = [early[0]] + [late[2 + f] for f in range(frame_count - 1)]
    first_hist = tuple(with_rim(early[1 + k], 0, span_count) for k in range(2))
    second_hist = tuple(with_rim(late[k], 0, span_count) for k in range(2))
    local_taps = (arrange_taps(conv_weight[0, 0]), arrange_taps(conv_weight[0, 1]))
    incoming = jnp.zeros_like(frames_span[0])
    produced = [jnp.zeros_like(frames_span[0]) for _ in range(frame_count)]
    tick_count = frame_count + phase_count - 1
    for tick_no in range(tick_count):
        frame_no = tick_no - phase_no
        active_now = jnp.logical_and(frame_no >= 0, frame_no < frame_count)
        source = jnp.where(phase_no == 0, frames_span[min(tick_no, frame_count - 1)], incoming)
        result, first_next, second_next = run_frame(
            source, first_hist, second_hist, local_taps, conv_bias[0], norm_gain[0], norm_shift[0],
            cell_count, span_count,
        )
        first_hist = tuple(jnp.where(active_now, a, b) for a, b in zip(first_next, first_hist))
        second_hist = tuple(jnp.where(active_now, a, b) for a, b in zip(second_next, second_hist))
        for f in range(frame_count):
            if 0 <= tick_no - f < phase_count:
                produced[f] = jnp.where(frame_no == f, result, produced[f])
        if tick_no + 1 < tick_count:
            incoming = pass_on(result, span_count)
    start = (lax.axis_index("rows") % span_count) * rows_here
    rim = 1 if padded else 0
    produced = jnp.stack([lax.dynamic_slice_in_dim(p, start, rows_here, axis=0) for p in produced])
    new_cache = jnp.stack(
        [
            jnp.stack([lax.dynamic_slice_in_dim(h, start + rim, rows_here, axis=0) for h in hist])
            for hist in (first_hist, second_hist)
        ]
    )
    produced = jnp.transpose(produced, (0, 2, 1, 3))
    new_cache = jnp.transpose(new_cache, (0, 1, 3, 2, 4))
    return (produced[None], new_cache[None])


def solution(mesh):
    in_specs = (
        P(None, None, "rows", None),
        P("phase", None, None, None, "rows", None),
        P("phase", None, None, None, None, None, None),
        P("phase", None, None),
        P("phase", None, None),
        P("phase", None, None),
    )
    out_specs = (P("phase", None, None, "rows", None), P("phase", None, None, None, "rows", None))
    return jax.shard_map(shards, mesh=mesh, in_specs=in_specs, out_specs=out_specs, check_vma=False)
```

profile of v0, /device:TPU:4, one launch (start us, length us, event | category | flops | bytes accessed | tf_op | source)
XLA Modules:
  0.0 245.1 jit_solution(8041478604036144962)
XLA Ops:
  7.2 1.0 copy.83
  8.2 1.1 copy.82
  10.9 4.7 %slice_bitcast_fusion = (bf16[3,192,3,3,192]{4,1,0,3,2:T(8,128)(2,1)}, bf16[3,192,3,3,192]{4,1,0,3,2:T(8,128)(2,1)S(1)}) fusion(bf16[1,2,3,3,3,192,192]{6,5,4,3,2,1,0:T(8,128)(2,1)} %param.23), kind=kLoop, calls=%fused_computation | loop fusion | bytes 7962624 | tf_op jit(solution)/shard_map/transpose | solution.py:77
  15.6 2.3 copy.31
  17.9 4.6 %reshape.38.taps = bf16[576,1728]{1,0:T(8,128)(2,1)} reshape(bf16[3,192,3,3,192]{4,3,2,1,0:T(4,128)(2,1)S(1)} %copy.31) | data formatting | bytes 3981312 | tf_op jit(solution)/shard_map/reshape | solution.py:77
  22.5 0.8 copy.36.bias
  23.3 0.8 copy.37.gain
  24.0 0.8 copy.38.shift
  24.8 1.3 concatenate.68.flags
  26.7 4.0 %copy.32 = bf16[3,192,3,3,192]{4,3,2,1,0:T(4,128)(2,1)S(1)} copy(bf16[3,192,3,3,192]{4,1,0,3,2:T(8,128)(2,1)} %get-tuple-element.62) | data formatting | bytes 3981312 | tf_op jit(solution)/shard_map/transpose | solution.py:77
  30.8 4.2 %reshape.39.taps = bf16[576,1728]{1,0:T(8,128)(2,1)} reshape(bf16[3,192,3,3,192]{4,3,2,1,0:T(4,128)(2,1)S(1)} %copy.32) | data formatting | bytes 3981312 | tf_op jit(solution)/shard_map/reshape | solution.py:77
  35.0 0.8 copy.33.bias
  35.8 0.8 copy.34.gain
  36.6 0.8 copy.35.shift
  37.3 0.8 compare_convert_fusion.member
  38.1 4.9 %all-gather.5.cloned.1.call-done.caches.frames = bf16[3,16,192,128]{3,2,1,0:T(8,128)(2,1)} async-done(((bf16[3,2,192,128]{3,2,1,0:T(8,128)(2,1)}), bf16[3,16,192,128]{3,2,1,0:T(8,128)(2,1)}) %all-gather.5.cloned.1.call-update) | async-done | bytes 2359312 | tf_op jit(solution)/shard_map/all_gather | solution.py:332
  43.0 1.1 broadcast_in_dim.8.a_p.a_pp
  44.1 0.8 broadcast_in_dim.9.src_b.src_c
  44.9 11.4 %shard_map.212 = (bf16[16,192,128]{2,1,0:T(8,128)(2,1)}, bf16[18,192,128]{2,1,0:T(8,128)(2,1)}) custom-call(s32[7]{0:T(128)} %concatenate.69.flags, bf16[3,16,192,128]{3,2,1,0:T(8,128)(2,1)} %all-gather.5.cloned.1.call-done.caches.frames, bf16[18,192,128]{2,1,0:T(8,128)(2,1)} %broadcast_in_dim.8.a_p.a_pp, bf16[18,192,128]{2,1,0:T(8,128)(2,1)} %broadcast_in_dim.8.a_p.a_pp, ...), custom_call_target="tpu_custom_call" | custom-call | tf_op jit(solution)/shard_map/pallas_call | solution.py:277
  56.4 19.1 %all-gather.3.cloned.1.call-done.caches.frames = bf16[3,16,192,128]{3,2,1,0:T(8,128)(2,1)} async-done(((bf16[3,2,192,128]{3,2,1,0:T(8,128)(2,1)}), bf16[3,16,192,128]{3,2,1,0:T(8,128)(2,1)}) %all-gather.3.cloned.1.call-update) | async-done | bytes 2359312 | tf_op jit(solution)/shard_map/all_gather | solution.py:333
  75.4 7.5 %shard_map.213 = (bf16[8,192,128]{2,1,0:T(8,128)(2,1)}, bf16[18,192,128]{2,1,0:T(8,128)(2,1)}) custom-call(s32[7]{0:T(128)} %concatenate.68.flags, bf16[3,16,192,128]{3,2,1,0:T(8,128)(2,1)} %all-gather.3.cloned.1.call-done.caches.frames, bf16[18,192,128]{2,1,0:T(8,128)(2,1)} %broadcast_in_dim.8.a_p.a_pp, bf16[18,192,128]{2,1,0:T(8,128)(2,1)} %broadcast_in_dim.8.a_p.a_pp, ...), custom_call_target="tpu_custom_call" | custom-call | tf_op jit(solution)/shard_map/pallas_call | solution.py:277
  82.9 3.4 %collective-permute-start = (bf16[8,192,128]{2,1,0:T(8,128)(2,1)}, bf16[8,192,128]{2,1,0:T(8,128)(2,1)S(1)}, u32[]{:S(2)}, u32[]{:S(2)}) collective-permute-start(bf16[8,192,128]{2,1,0:T(8,128)(2,1)} %get-tuple-element.32), channel_id=1, source_target_pairs={{0,8},{8,16},{16,24},{1,9},{9,17},{17,25},{2,10},{10,18},{18,26},{... | collective-permute-start | bytes 1179656 | tf_op jit(solution)/shard_map/ppermute | solution.py:369
  86.3 7.8 %shard_map.214 = bf16[8,192,128]{2,1,0:T(8,128)(2,1)} custom-call(s32[7]{0:T(128)} %concatenate.68.flags, bf16[3,16,192,128]{3,2,1,0:T(8,128)(2,1)} %all-gather.3.cloned.1.call-done.caches.frames, bf16[18,192,128]{2,1,0:T(8,128)(2,1)} %broadcast_in_dim.8.a_p.a_pp, bf16[18,192,128]{2,1,0:T(8,128)(2,1)} %broadcast_in_dim.8.a_p.a_pp, ...), custom_call_target="tpu_custom_call" | custom-call | tf_op jit(solution)/shard_map/pallas_call | solution.py:277
  94.1 3.1 %collective-permute-done.src_b = bf16[8,192,128]{2,1,0:T(8,128)(2,1)S(1)} collective-permute-done((bf16[8,192,128]{2,1,0:T(8,128)(2,1)}, bf16[8,192,128]{2,1,0:T(8,128)(2,1)S(1)}, u32[]{:S(2)}, u32[]{:S(2)}) %collective-permute-start) | collective-permute-done | bytes 393248 | tf_op jit(solution)/shard_map/ppermute | solution.py:369
  99.6 11.1 %shard_map.215 = (bf16[16,192,128]{2,1,0:T(8,128)(2,1)}, bf16[18,192,128]{2,1,0:T(8,128)(2,1)}) custom-call(s32[7]{0:T(128)} %concatenate.71.flags, bf16[3,16,192,128]{3,2,1,0:T(8,128)(2,1)} %all-gather.5.cloned.1.call-done.caches.frames, bf16[18,192,128]{2,1,0:T(8,128)(2,1)} %get-tuple-element.34.a_p.a_pp, bf16[18,192,128]{2,1,0:T(8,128)(2,1)} %broadcast_in_dim.8.a_p.a_pp, ...), custom_call_target="tpu_custom_call" | custom-call | tf_op jit(solution)/shard_map/pallas_call | solution.py:277
  110.7 7.5 %shard_map.216 = (bf16[8,192,128]{2,1,0:T(8,128)(2,1)}, bf16[18,192,128]{2,1,0:T(8,128)(2,1)}) custom-call(s32[7]{0:T(128)} %concatenate.67.flags, bf16[3,16,192,128]{3,2,1,0:T(8,128)(2,1)} %all-gather.3.cloned.1.call-done.caches.frames, bf16[18,192,128]{2,1,0:T(8,128)(2,1)} %get-tuple-element.31.rest_0_.a_p.a_pp, ...), custom_call_target="tpu_custom_call" | custom-call | tf_op jit(solution)/shard_map/pallas_call | solution.py:277
  118.2 2.5 %collective-permute-start.2 = (bf16[8,192,128]{2,1,0:T(8,128)(2,1)}, bf16[8,192,128]{2,1,0:T(8,128)(2,1)S(1)}, u32[]{:S(2)}, u32[]{:S(2)}) collective-permute-start(bf16[8,192,128]{2,1,0:T(8,128)(2,1)} %get-tuple-element.37), channel_id=1, source_target_pairs={{0,8},{8,16},{16,24},{1,9},{9,17},{17,25},{2,10},{10,18},{18,26},{... | collective-permute-start | bytes 1179656 | tf_op jit(solution)/shard_map/ppermute | solution.py:369
  120.7 7.3 %shard_map.217 = bf16[8,192,128]{2,1,0:T(8,128)(2,1)} custom-call(s32[7]{0:T(128)} %concatenate.67.flags, bf16[3,16,192,128]{3,2,1,0:T(8,128)(2,1)} %all-gather.3.cloned.1.call-done.caches.frames, bf16[18,192,128]{2,1,0:T(8,128)(2,1)} %get-tuple-element.31.rest_0_.a_p.a_pp, bf16[18,192,128]{2,1,0:T(8,128)(2,1)} %broadcast_in_dim.8.a_p.a_pp, ...), custom_call_target="tpu_custom_call" | custom-call | tf_op jit(solution)/shard_map/pallas_call | solution.py:277
  128.0 4.4 %collective-permute-done.2.src_b = bf16[8,192,128]{2,1,0:T(8,128)(2,1)S(1)} collective-permute-done((bf16[8,192,128]{2,1,0:T(8,128)(2,1)}, bf16[8,192,128]{2,1,0:T(8,128)(2,1)S(1)}, u32[]{:S(2)}, u32[]{:S(2)}) %collective-permute-start.2) | collective-permute-done | bytes 393248 | tf_op jit(solution)/shard_map/ppermute | solution.py:369
  134.8 11.1 %shard_map.218 = (bf16[16,192,128]{2,1,0:T(8,128)(2,1)}, bf16[18,192,128]{2,1,0:T(8,128)(2,1)}) custom-call(s32[7]{0:T(128)} %concatenate.73.flags, bf16[3,16,192,128]{3,2,1,0:T(8,128)(2,1)} %all-gather.5.cloned.1.call-done.caches.frames, bf16[18,192,128]{2,1,0:T(8,128)(2,1)} %get-tuple-element.39.a_p.a_pp, ...), custom_call_target="tpu_custom_call" | custom-call | tf_op jit(solution)/shard_map/pallas_call | solution.py:277
  146.0 7.5 %shard_map.219 = (bf16[8,192,128]{2,1,0:T(8,128)(2,1)}, bf16[18,192,128]{2,1,0:T(8,128)(2,1)}) custom-call(s32[7]{0:T(128)} %concatenate.66.flags, bf16[3,16,192,128]{3,2,1,0:T(8,128)(2,1)} %all-gather.3.cloned.1.call-done.caches.frames, bf16[18,192,128]{2,1,0:T(8,128)(2,1)} %get-tuple-element.36.rest_0_.a_p.a_pp, ...), custom_call_target="tpu_custom_call" | custom-call | tf_op jit(solution)/shard_map/pallas_call | solution.py:277
  153.4 1.9 collective-permute-start.4
  155.4 7.3 %shard_map.220 = bf16[8,192,128]{2,1,0:T(8,128)(2,1)} custom-call(s32[7]{0:T(128)} %concatenate.66.flags, bf16[3,16,192,128]{3,2,1,0:T(8,128)(2,1)} %all-gather.3.cloned.1.call-done.caches.frames, bf16[18,192,128]{2,1,0:T(8,128)(2,1)} %get-tuple-element.36.rest_0_.a_p.a_pp, bf16[18,192,128]{2,1,0:T(8,128)(2,1)} %get-tuple-element.31.rest_0_.a_p.a_pp, ...), custom_call_target="tpu_custom_call" | custom-call | tf_op jit(solution)/shard_map/pallas_call | solution.py:277
  162.7 4.9 %collective-permute-done.4.src_b = bf16[8,192,128]{2,1,0:T(8,128)(2,1)S(1)} collective-permute-done((bf16[8,192,128]{2,1,0:T(8,128)(2,1)}, bf16[8,192,128]{2,1,0:T(8,128)(2,1)S(1)}, u32[]{:S(2)}, u32[]{:S(2)}) %collective-permute-start.4) | collective-permute-done | bytes 393248 | tf_op jit(solution)/shard_map/ppermute | solution.py:369
  170.1 11.1 %shard_map.221 = (bf16[16,192,128]{2,1,0:T(8,128)(2,1)}, bf16[18,192,128]{2,1,0:T(8,128)(2,1)}) custom-call(s32[7]{0:T(128)} %concatenate.75.flags, bf16[3,16,192,128]{3,2,1,0:T(8,128)(2,1)} %all-gather.5.cloned.1.call-done.caches.frames, bf16[18,192,128]{2,1,0:T(8,128)(2,1)} %get-tuple-element.44.a_p.a_pp, ...), custom_call_target="tpu_custom_call" | custom-call | tf_op jit(solution)/shard_map/pallas_call | solution.py:277
  181.2 7.5 %shard_map.222 = (bf16[8,192,128]{2,1,0:T(8,128)(2,1)}, bf16[18,192,128]{2,1,0:T(8,128)(2,1)}) custom-call(s32[7]{0:T(128)} %concatenate.65.flags, bf16[3,16,192,128]{3,2,1,0:T(8,128)(2,1)} %all-gather.3.cloned.1.call-done.caches.frames, bf16[18,192,128]{2,1,0:T(8,128)(2,1)} %get-tuple-element.41.rest_0_.a_p.a_pp, ...), custom_call_target="tpu_custom_call" | custom-call | tf_op jit(solution)/shard_map/pallas_call | solution.py:277
  188.6 1.9 collective-permute-start.6
  190.6 7.4 %shard_map.223 = bf16[8,192,128]{2,1,0:T(8,128)(2,1)} custom-call(s32[7]{0:T(128)} %concatenate.65.flags, bf16[3,16,192,128]{3,2,1,0:T(8,128)(2,1)} %all-gather.3.cloned.1.call-done.caches.frames, bf16[18,192,128]{2,1,0:T(8,128)(2,1)} %get-tuple-element.41.rest_0_.a_p.a_pp, bf16[18,192,128]{2,1,0:T(8,128)(2,1)} %get-tuple-element.36.rest_0_.a_p.a_pp, ...), custom_call_target="tpu_custom_call" | custom-call | tf_op jit(solution)/shard_map/pallas_call | solution.py:277
  198.0 4.8 %collective-permute-done.6.src_b = bf16[8,192,128]{2,1,0:T(8,128)(2,1)S(1)} collective-permute-done((bf16[8,192,128]{2,1,0:T(8,128)(2,1)}, bf16[8,192,128]{2,1,0:T(8,128)(2,1)S(1)}, u32[]{:S(2)}, u32[]{:S(2)}) %collective-permute-start.6) | collective-permute-done | bytes 393248 | tf_op jit(solution)/shard_map/ppermute | solution.py:369
  204.1 1.8 select_bitcast_fusion.3
  206.6 11.1 %shard_map.224 = (bf16[16,192,128]{2,1,0:T(8,128)(2,1)}, bf16[18,192,128]{2,1,0:T(8,128)(2,1)}) custom-call(s32[7]{0:T(128)} %concatenate.78.flags, bf16[3,16,192,128]{3,2,1,0:T(8,128)(2,1)} %all-gather.5.cloned.1.call-done.caches.frames, bf16[18,192,128]{2,1,0:T(8,128)(2,1)} %get-tuple-element.53.a_p, bf16[18,192,128]{2,1,0:T(8,128)(2,1)} %get-tuple-element.44.a_p.a_pp, ...), custom_call_target="tpu_custom_call" | custom-call | tf_op jit(solution)/shard_map/pallas_call | solution.py:277
  217.7 7.5 %shard_map.225 = (bf16[8,192,128]{2,1,0:T(8,128)(2,1)}, bf16[18,192,128]{2,1,0:T(8,128)(2,1)}) custom-call(s32[7]{0:T(128)} %concatenate.77.flags, bf16[3,16,192,128]{3,2,1,0:T(8,128)(2,1)} %all-gather.3.cloned.1.call-done.caches.frames, bf16[18,192,128]{2,1,0:T(8,128)(2,1)} %get-tuple-element.47.rest_0_.a_p, ...), custom_call_target="tpu_custom_call" | custom-call | tf_op jit(solution)/shard_map/pallas_call | solution.py:277
  225.2 7.2 %shard_map.226 = bf16[8,192,128]{2,1,0:T(8,128)(2,1)} custom-call(s32[7]{0:T(128)} %concatenate.77.flags, bf16[3,16,192,128]{3,2,1,0:T(8,128)(2,1)} %all-gather.3.cloned.1.call-done.caches.frames, bf16[18,192,128]{2,1,0:T(8,128)(2,1)} %get-tuple-element.47.rest_0_.a_p, bf16[18,192,128]{2,1,0:T(8,128)(2,1)} %get-tuple-element.41.rest_0_.a_p.a_pp, ...), custom_call_target="tpu_custom_call" | custom-call | tf_op jit(solution)/shard_map/pallas_call | solution.py:277
  232.4 1.1 select_bitcast_fusion.2
  233.6 0.9 copy.78
  234.5 1.1 fusion.1
  235.6 1.1 fusion.7
  236.9 1.2 copy.79
  (71 shorter events, 11.9 us)
Async XLA Ops:
  7.2 35.9 %all-gather.5.cloned.1.call-start = ((), (), s32[]{:S(2)}) async-start(), calls=%async_computation.1 | async-start | bytes 2654208 | tf_op jit(solution)/shard_map/all_gather | solution.py:332
  10.1 65.4 %all-gather.3.cloned.1.call-start = ((), (), s32[]{:S(2)}) async-start(), calls=%async_computation | async-start | bytes 2654208 | tf_op jit(solution)/shard_map/all_gather | solution.py:333
  17.8 4.7 %copy-start.14 = (f32[1,2,192]{2,1,0:T(2,128)S(1)}, f32[1,2,192]{2,1,0:T(2,128)}, u32[]{:S(2)}) copy-start(f32[1,2,192]{2,1,0:T(2,128)} %param.24) | copy-start | bytes 4612
  17.9 5.4 %copy-start.15 = (f32[1,2,192]{2,1,0:T(2,128)S(1)}, f32[1,2,192]{2,1,0:T(2,128)}, u32[]{:S(2)}) copy-start(f32[1,2,192]{2,1,0:T(2,128)} %param.25) | copy-start | bytes 4612
  17.9 6.2 %copy-start.16 = (f32[1,2,192]{2,1,0:T(2,128)S(1)}, f32[1,2,192]{2,1,0:T(2,128)}, u32[]{:S(2)}) copy-start(f32[1,2,192]{2,1,0:T(2,128)} %param.26) | copy-start | bytes 4612
  82.9 14.3 %collective-permute-start = (bf16[8,192,128]{2,1,0:T(8,128)(2,1)}, bf16[8,192,128]{2,1,0:T(8,128)(2,1)S(1)}, u32[]{:S(2)}, u32[]{:S(2)}) collective-permute-start(bf16[8,192,128]{2,1,0:T(8,128)(2,1)} %get-tuple-element.32), channel_id=1, source_target_pairs={{0,8},{8,16},{16,24},{1,9},{9,17},{17,25},{2,10},{10,18},{18,26},{... | collective-permute-start | bytes 1179656 | tf_op jit(solution)/shard_map/ppermute | solution.py:369
  86.3 10.9 %copy-start.13 = (s32[3]{0:T(128)S(1)}, s32[3]{0:T(128)}, u32[]{:S(2)}) copy-start(s32[3]{0:T(128)} %constant.106.clone) | copy-start | bytes 40
  86.3 11.6 %copy-start.12 = (s32[3]{0:T(128)S(1)}, s32[3]{0:T(128)}, u32[]{:S(2)}) copy-start(s32[3]{0:T(128)} %constant.105.clone) | copy-start | bytes 40
  97.1 1.7 copy-start.3
  97.1 1.7 collective-permute-start.1
  98.9 0.7 copy-start.5
  118.2 14.2 %collective-permute-start.2 = (bf16[8,192,128]{2,1,0:T(8,128)(2,1)}, bf16[8,192,128]{2,1,0:T(8,128)(2,1)S(1)}, u32[]{:S(2)}, u32[]{:S(2)}) collective-permute-start(bf16[8,192,128]{2,1,0:T(8,128)(2,1)} %get-tuple-element.37), channel_id=1, source_target_pairs={{0,8},{8,16},{16,24},{1,9},{9,17},{17,25},{2,10},{10,18},{18,26},{... | collective-permute-start | bytes 1179656 | tf_op jit(solution)/shard_map/ppermute | solution.py:369
  132.4 1.7 copy-start.2
  132.4 1.7 collective-permute-start.3
  134.1 0.8 copy-start.6
  153.4 14.2 %collective-permute-start.4 = (bf16[8,192,128]{2,1,0:T(8,128)(2,1)}, bf16[8,192,128]{2,1,0:T(8,128)(2,1)S(1)}, u32[]{:S(2)}, u32[]{:S(2)}) collective-permute-start(bf16[8,192,128]{2,1,0:T(8,128)(2,1)} %get-tuple-element.42), channel_id=1, source_target_pairs={{0,8},{8,16},{16,24},{1,9},{9,17},{17,25},{2,10},{10,18},{18,26},{... | collective-permute-start | bytes 1179656 | tf_op jit(solution)/shard_map/ppermute | solution.py:369
  167.6 1.7 copy-start.4
  167.6 1.7 collective-permute-start.5
  169.3 0.7 copy-start.7
  188.6 14.2 %collective-permute-start.6 = (bf16[8,192,128]{2,1,0:T(8,128)(2,1)}, bf16[8,192,128]{2,1,0:T(8,128)(2,1)S(1)}, u32[]{:S(2)}, u32[]{:S(2)}) collective-permute-start(bf16[8,192,128]{2,1,0:T(8,128)(2,1)} %get-tuple-element.46), channel_id=1, source_target_pairs={{0,8},{8,16},{16,24},{1,9},{9,17},{17,25},{2,10},{10,18},{18,26},{... | collective-permute-start | bytes 1179656 | tf_op jit(solution)/shard_map/ppermute | solution.py:369
  197.9 6.1 %copy-start.8 = (bf16[8,192,128]{2,1,0:T(8,128)(2,1)S(1)}, bf16[8,192,128]{2,1,0:T(8,128)(2,1)}, u32[]{:S(2)}) copy-start(bf16[8,192,128]{2,1,0:T(8,128)(2,1)} %shard_map.217) | copy-start | bytes 1179652
  197.9 6.1 %copy-start.9 = (bf16[8,192,128]{2,1,0:T(8,128)(2,1)S(1)}, bf16[8,192,128]{2,1,0:T(8,128)(2,1)}, u32[]{:S(2)}) copy-start(bf16[8,192,128]{2,1,0:T(8,128)(2,1)} %shard_map.220) | copy-start | bytes 1179652
  198.0 6.1 %copy-start.10 = (bf16[8,192,128]{2,1,0:T(8,128)(2,1)S(1)}, bf16[8,192,128]{2,1,0:T(8,128)(2,1)}, u32[]{:S(2)}) copy-start(bf16[8,192,128]{2,1,0:T(8,128)(2,1)} %shard_map.223) | copy-start | bytes 1179652
  202.8 3.0 %copy-start = (bf16[8,192,128]{2,1,0:T(8,128)(2,1)}, bf16[8,192,128]{2,1,0:T(8,128)(2,1)S(1)}, u32[]{:S(2)}) copy-start(bf16[8,192,128]{2,1,0:T(8,128)(2,1)S(1)} %collective-permute-done.6.src_b) | copy-start | bytes 1179652
  202.8 3.0 %collective-permute-start.7 = (bf16[8,192,128]{2,1,0:T(8,128)(2,1)S(1)}, bf16[8,192,128]{2,1,0:T(8,128)(2,1)S(1)}, u32[]{:S(2)}, u32[]{:S(2)}) collective-permute-start(bf16[8,192,128]{2,1,0:T(8,128)(2,1)S(1)} %collective-permute-done.6.src_b), channel_id=1, source_target_pairs={{0,1},{1,0},{2,3},{3,2},{4,5},{5,4},{6,7},{7,6},{8,9},{9,8},{10,11... | collective-permute-start | bytes 1179656 | tf_op jit(solution)/shard_map/ppermute | solution.py:371
  205.8 0.8 copy-start.1
  225.2 8.4 %copy-start.11 = (bf16[1,2,192,128]{3,2,1,0:T(8,128)(2,1)S(1)}, bf16[1,2,192,128]{3,2,1,0:T(8,128)(2,1)}, u32[]{:S(2)}) copy-start(bf16[1,2,192,128]{3,2,1,0:T(8,128)(2,1)} %select_bitcast_fusion.3) | copy-start | bytes 294916
  225.2 9.3 %slice-start = ((bf16[3,16,192,128]{3,2,1,0:T(8,128)(2,1)}), bf16[1,16,192,128]{3,2,1,0:T(8,128)(2,1)S(1)}, s32[]{:S(2)}) async-start(bf16[3,16,192,128]{3,2,1,0:T(8,128)(2,1)} %all-gather.3.cloned.1.call-done.caches.frames), calls=%async_computation.2 | async-start | bytes 1572864 | tf_op jit(solution)/shard_map/slice | solution.py:375
  225.2 10.4 %slice-start.1 = ((bf16[3,16,192,128]{3,2,1,0:T(8,128)(2,1)}), bf16[1,16,192,128]{3,2,1,0:T(8,128)(2,1)S(1)}, s32[]{:S(2)}) async-start(bf16[3,16,192,128]{3,2,1,0:T(8,128)(2,1)} %all-gather.5.cloned.1.call-done.caches.frames), calls=%async_computation.3 | async-start | bytes 1572864 | tf_op jit(solution)/shard_map/slice | solution.py:375
Sparse Core Ops, SparseCore 0:
  10.2 32.8 all-gather.4
  44.6 30.7 all-gather.2
where the time goes:
time: 250 us; the launch traced here: 245 us
  Pallas kernels  130 us (52%)
  waiting for transfers between devices  42.5 us (17%)
  local copies, waits for them, and re-layouts  40.5 us (16%)
  between operations  14.7 us (6%)
  starting transfers between devices  9.77 us (4%)
  other arithmetic  7.57 us (3%)
    pallas_call x15, Pallas kernels, fused_conv(): pl.pallas_call(body, out_shape=shapes, in_specs=specs, out_specs=vmem if...  130 us
    all_gather x1, waiting for transfers between devices, shards_whole(): lax.all_gather(jnp.stack([cache_t[1, 0], cache_t[1, 1]] + list(frames_t[1...  19.1 us
    ppermute x4, waiting for transfers between devices, shards_whole(): got = lax.ppermute(lead, 'phase', forward)  17.2 us
    transpose x3, local copies, waits for them, and re-layouts, arrange_taps(): jnp.transpose(weight, (2, 3, 0, 1, 4)).reshape(3 * outputs, 9 * channels)  11 us
    ppermute x4, starting transfers between devices, shards_whole(): got = lax.ppermute(lead, 'phase', forward)  9.68 us
    reshape x2, local copies, waits for them, and re-layouts, arrange_taps(): jnp.transpose(weight, (2, 3, 0, 1, 4)).reshape(3 * outputs, 9 * channels)  8.86 us
    unnamed x38, local copies, waits for them, and re-layouts  7.09 us
    concatenate x10, local copies, waits for them, and re-layouts, fused_conv(): jnp.concatenate([flags[:3], jnp.array([frame_at, cache_at[0], cache_at[1]...  7.03 us
  transfers between devices with their start and end apart: 10, of which 9 were waited for; matrix products, arithmetic and copies ran while one was open for 15% of the time, Pallas kernels for 17%

commit v1 on v0

--- a/solution.py
+++ b/solution.py
@@ -160,7 +160,8 @@
     lax.fori_loop(0, count // pair, step, 0)
 
 
-def fused_body(flags, caches, a_p, a_pp, frames, src_b, src_c, taps, bias, member, gain, shift, *rest, kind):
+def fused_body(flags, caches, a_p, a_pp, frames, src_b, src_c, taps, bias, member, gain, shift, *rest,
+               kind, tick, frame_at, cache_at):
     rest = list(rest)
     own = rest.pop(0) if kind != "first" else None
     if kind == "tail":
@@ -170,9 +171,9 @@
         out, act, x0, x1, rawbuf, sems = rest
     span, channels, columns = rawbuf.shape
     half = span // 2
-    first, second, mode, core = flags[0], flags[1], flags[2], flags[6]
-    c0, c1 = caches.at[flags[4]], caches.at[flags[5]]
-    whole = frames.at[flags[3]]
+    first, second, mode, core = flags[tick, 0], flags[tick, 1], flags[tick, 2], flags[tick, 3]
+    c0, c1 = caches.at[cache_at[0]], caches.at[cache_at[1]]
+    whole = frames.at[frame_at]
     top, bottom = rawbuf.at[pl.ds(0, half)], rawbuf.at[pl.ds(half, half)]
     inner0, inner1 = x0.at[pl.ds(1, span)], x1.at[pl.ds(1, span)]
 
@@ -254,14 +255,13 @@
         conv_span(x0, x1, act, taps, bias, rawbuf, out, base, half)
 
 
-def fused_conv(flags, caches, cache_at, recent, frames, frame_at, halves, taps, bias_vec, norm, kind, own=None):
+def fused_conv(flags, tick, caches, cache_at, recent, frames, frame_at, halves, taps, bias_vec, norm, kind, own=None):
     span, channels, columns = caches.shape[1:]
     outputs = taps.shape[0] // 3
     group_of = jnp.arange(channels) // (channels // GROUPS)
     member = (group_of[:, None] == group_of[None, :]).astype(jnp.float32)
     vmem = pl.BlockSpec(memory_space=pltpu.VMEM)
     anywhere = pl.BlockSpec(memory_space=pl.ANY)
-    flags = jnp.concatenate([flags[:3], jnp.array([frame_at, cache_at[0], cache_at[1]], jnp.int32), flags[3:]])
     args = [flags, caches, recent[0], recent[1], frames, halves[0], halves[1]]
     args += [taps, bias_vec.reshape(outputs, 1), member]
     args += [v.reshape(-1, 1).astype(jnp.float32) for v in norm]
@@ -273,7 +273,9 @@
     result = jax.ShapeDtypeStruct((rows_out, outputs, columns), jnp.bfloat16)
     padded = jax.ShapeDtypeStruct((span + 2, channels, columns), jnp.bfloat16)
     shapes = result if kind == "tail" else (result, padded)
-    body = functools.partial(fused_body, kind=kind)
+    body = functools.partial(
+        fused_body, kind=kind, tick=tick, frame_at=frame_at, cache_at=tuple(cache_at)
+    )
     return pl.pallas_call(
         body,
         out_shape=shapes,
@@ -330,11 +332,13 @@
     frames_t = jnp.transpose(frames, (0, 2, 1, 3))
     cache_t = jnp.transpose(causal_cache[0], (0, 1, 3, 2, 4))
     early = lax.all_gather(jnp.stack([frames_t[0], cache_t[0, 0], cache_t[0, 1]]), "rows", axis=1, tiled=True)
-    late = lax.all_gather(
-        jnp.stack([cache_t[1, 0], cache_t[1, 1]] + list(frames_t[1:])), "rows", axis=1, tiled=True
-    )
-    frame_of = [(early, 0)] + [(late, 2 + f) for f in range(frame_count - 1)]
-    cache_of = ((early, (1, 2)), (late, (0, 1)))
+    second_cache = lax.all_gather(cache_t[1], "rows", axis=1, tiled=True)
+    later = list(frames_t[1:])
+    if len(later) == 1:
+        later = later * 2
+    later = lax.all_gather(jnp.stack(later), "rows", axis=1, tiled=True) if later else early
+    frame_of = [(early, 0)] + [(later, f) for f in range(frame_count - 1)]
+    cache_of = ((early, (1, 2)), (second_cache, (0, 1)))
     taps = (arrange_taps(conv_weight[0, 0]), arrange_taps(conv_weight[0, 1]))
 
     def own_rows(x, rim=0):
@@ -348,9 +352,12 @@
     kept = [[blank, blank], [blank, blank]]
     mode = jnp.where(phase_no == 0, 0, 1 + core)
     tick_count = frame_count + phase_count - 1
+    frame_nos = jnp.arange(tick_count) - phase_no
+    flags = jnp.stack(
+        [frame_nos == 0, frame_nos == 1, jnp.full((tick_count,), mode), jnp.full((tick_count,), core)], axis=1
+    ).astype(jnp.int32)
     for tick_no in range(tick_count):
         frame_no = tick_no - phase_no
-        flags = jnp.stack([frame_no == 0, frame_no == 1, mode, core]).astype(jnp.int32)
         frame_stack, frame_at = frame_of[min(tick_no, frame_count - 1)]
         recents = []
         for j in range(2):
@@ -359,10 +366,10 @@
             recents.append((a_p, a_pp))
         common = (frame_stack, frame_at, (got, other))
         hidden, first_in = fused_conv(
-            flags, cache_of[0][0], cache_of[0][1], recents[0], *common,
+            flags, tick_no, cache_of[0][0], cache_of[0][1], recents[0], *common,
             taps[0], conv_bias[0, 0], (norm_gain[0, 0], norm_shift[0, 0]), "first",
         )
-        second = (flags, cache_of[1][0], cache_of[1][1], recents[1], *common, taps[1], conv_bias[0, 1])
+        second = (flags, tick_no, cache_of[1][0], cache_of[1][1], recents[1], *common, taps[1], conv_bias[0, 1])
         lead, second_in = fused_conv(*second, (norm_gain[0, 1], norm_shift[0, 1]), "lead", hidden)
         tail = fused_conv(*second, (norm_gain[0, 1], norm_shift[0, 1]), "tail", second_in)
         if tick_no + 1 < tick_count:

time: 250 us -> 245 us (0.980)
  local copies, waits for them, and re-layouts: 40.5 us -> 35.4 us
    concatenate x10 -> x0, local copies, waits for them, and re-layouts: 7.03 us -> none  [fused_conv(): jnp.concatenate([flags[:3], jnp.array([frame_at, cache_at[0], cache_at[1]...]
    all_gather x1 -> x2, waiting for transfers between devices: 19.1 us -> 17.6 us  [the longest x1 13.1 us: shards_whole(): second_cache = lax.all_gather(cache_t[1], 'rows', axis=1, tiled=True)]
    unnamed x38 -> x32, local copies, waits for them, and re-layouts: 7.09 us -> 7.07 us
  transfers between devices with their start and end apart: 10 -> 11, of which waited for: 9 -> 10; matrix products, arithmetic and copies ran while one was open for 15% -> 13% of each run, Pallas kernels for 17% -> 20%
where the time goes in v1:
time: 245 us; the launch traced here: 240 us
  Pallas kernels  130 us (53%)
  waiting for transfers between devices  40.8 us (17%)
  local copies, waits for them, and re-layouts  35.4 us (14%)
  between operations  14.4 us (6%)
  starting transfers between devices  11.3 us (5%)
  other arithmetic  8.42 us (3%)
    pallas_call x15, Pallas kernels, fused_conv(): pl.pallas_call(body, out_shape=shapes, in_specs=specs, out_specs=vmem if...  130 us
    ppermute x4, waiting for transfers between devices, shards_whole(): got = lax.ppermute(lead, 'phase', forward)  15.7 us
    all_gather x1, waiting for transfers between devices, shards_whole(): second_cache = lax.all_gather(cache_t[1], 'rows', axis=1, tiled=True)  13.1 us
    ppermute x4, starting transfers between devices, shards_whole(): got = lax.ppermute(lead, 'phase', forward)  11.1 us
    transpose x3, local copies, waits for them, and re-layouts, arrange_taps(): jnp.transpose(weight, (2, 3, 0, 1, 4)).reshape(3 * outputs, 9 * channels)  11 us
    reshape x2, local copies, waits for them, and re-layouts, arrange_taps(): jnp.transpose(weight, (2, 3, 0, 1, 4)).reshape(3 * outputs, 9 * channels)  8.81 us
    unnamed x32, local copies, waits for them, and re-layouts  7.07 us
  transfers between devices with their start and end apart: 11, of which 10 were waited for; matrix products, arithmetic and copies ran while one was open for 13% of the time, Pallas kernels for 20%

profile of v1, /device:TPU:4, one launch (start us, length us, event | category | flops | bytes accessed | tf_op | source)
XLA Modules:
  0.0 240.5 jit_solution(11022825361493113545)
XLA Ops:
  7.2 1.0 copy.67
  8.3 1.0 copy.68
  12.8 4.7 %slice_bitcast_fusion = (bf16[3,192,3,3,192]{4,1,0,3,2:T(8,128)(2,1)S(1)}, bf16[3,192,3,3,192]{4,1,0,3,2:T(8,128)(2,1)}) fusion(bf16[1,2,3,3,3,192,192]{6,5,4,3,2,1,0:T(8,128)(2,1)} %param.8), kind=kLoop, calls=%fused_computation | loop fusion | bytes 7962624 | tf_op jit(solution)/shard_map/transpose | solution.py:77
  17.5 2.3 copy.17
  19.8 4.6 %reshape.59.taps = bf16[576,1728]{1,0:T(8,128)(2,1)} reshape(bf16[3,192,3,3,192]{4,3,2,1,0:T(4,128)(2,1)S(1)} %copy.17) | data formatting | bytes 3981312 | tf_op jit(solution)/shard_map/reshape | solution.py:77
  25.1 0.8 copy.19.gain
  26.7 4.0 %copy.16 = bf16[3,192,3,3,192]{4,3,2,1,0:T(4,128)(2,1)S(1)} copy(bf16[3,192,3,3,192]{4,1,0,3,2:T(8,128)(2,1)} %get-tuple-element.63) | data formatting | bytes 3981312 | tf_op jit(solution)/shard_map/transpose | solution.py:77
  30.7 4.2 %reshape.58.taps = bf16[576,1728]{1,0:T(8,128)(2,1)} reshape(bf16[3,192,3,3,192]{4,3,2,1,0:T(4,128)(2,1)S(1)} %copy.16) | data formatting | bytes 3981312 | tf_op jit(solution)/shard_map/reshape | solution.py:77
  35.7 0.8 copy.22.gain
  36.5 0.8 copy.23.shift
  37.3 1.3 add_add_fusion.flags
  38.6 0.8 compare_convert_fusion.member
  39.3 3.7 %all-gather.5.cloned.1.call-done.caches.frames = bf16[3,16,192,128]{3,2,1,0:T(8,128)(2,1)} async-done(((bf16[3,2,192,128]{3,2,1,0:T(8,128)(2,1)}), bf16[3,16,192,128]{3,2,1,0:T(8,128)(2,1)}) %all-gather.5.cloned.1.call-update) | async-done | bytes 2359312 | tf_op jit(solution)/shard_map/all_gather | solution.py:334
  43.0 1.1 broadcast_in_dim.8.a_p.a_pp
  44.1 0.8 broadcast_in_dim.9.src_b.src_c
  44.9 11.4 %shard_map.77 = (bf16[16,192,128]{2,1,0:T(8,128)(2,1)}, bf16[18,192,128]{2,1,0:T(8,128)(2,1)}) custom-call(s32[5,4]{1,0:T(8,128)} %add_add_fusion.flags, bf16[3,16,192,128]{3,2,1,0:T(8,128)(2,1)} %all-gather.5.cloned.1.call-done.caches.frames, bf16[18,192,128]{2,1,0:T(8,128)(2,1)} %broadcast_in_dim.8.a_p.a_pp, ...), custom_call_target="tpu_custom_call" | custom-call | tf_op jit(solution)/shard_map/pallas_call | solution.py:279
  56.4 13.1 %all-gather.9.cloned.1.call-done = bf16[1,2,16,192,128]{4,3,2,1,0:T(8,128)(2,1)} async-done(((bf16[1,2,2,192,128]{4,3,2,1,0:T(8,128)(2,1)}), bf16[1,2,16,192,128]{4,3,2,1,0:T(8,128)(2,1)}) %all-gather.9.cloned.1.call-update) | async-done | bytes 1572880 | tf_op jit(solution)/shard_map/all_gather | solution.py:335
  69.4 7.4 %shard_map.78 = (bf16[8,192,128]{2,1,0:T(8,128)(2,1)}, bf16[18,192,128]{2,1,0:T(8,128)(2,1)}) custom-call(s32[5,4]{1,0:T(8,128)} %add_add_fusion.flags, bf16[2,16,192,128]{3,2,1,0:T(8,128)(2,1)} %bitcast.111, bf16[18,192,128]{2,1,0:T(8,128)(2,1)} %broadcast_in_dim.8.a_p.a_pp, bf16[18,192,128]{2,1,0:T(8,128)(2,1)} %broadcast_in_dim.8.a_p.a_pp, ...), custom_call_target="tpu_custom_call" | custom-call | tf_op jit(solution)/shard_map/pallas_call | solution.py:279
  76.9 3.4 %collective-permute-start = (bf16[8,192,128]{2,1,0:T(8,128)(2,1)}, bf16[8,192,128]{2,1,0:T(8,128)(2,1)S(1)}, u32[]{:S(2)}, u32[]{:S(2)}) collective-permute-start(bf16[8,192,128]{2,1,0:T(8,128)(2,1)} %get-tuple-element.32), channel_id=1, source_target_pairs={{0,8},{8,16},{16,24},{1,9},{9,17},{17,25},{2,10},{10,18},{18,26},{... | collective-permute-start | bytes 1179656 | tf_op jit(solution)/shard_map/ppermute | solution.py:376
  80.3 7.9 %shard_map.79 = bf16[8,192,128]{2,1,0:T(8,128)(2,1)} custom-call(s32[5,4]{1,0:T(8,128)} %add_add_fusion.flags, bf16[2,16,192,128]{3,2,1,0:T(8,128)(2,1)} %bitcast.112, bf16[18,192,128]{2,1,0:T(8,128)(2,1)} %broadcast_in_dim.8.a_p.a_pp, bf16[18,192,128]{2,1,0:T(8,128)(2,1)} %broadcast_in_dim.8.a_p.a_pp, ...), custom_call_target="tpu_custom_call" | custom-call | tf_op jit(solution)/shard_map/pallas_call | solution.py:279
  88.1 3.0 %collective-permute-done.src_b = bf16[8,192,128]{2,1,0:T(8,128)(2,1)S(1)} collective-permute-done((bf16[8,192,128]{2,1,0:T(8,128)(2,1)}, bf16[8,192,128]{2,1,0:T(8,128)(2,1)S(1)}, u32[]{:S(2)}, u32[]{:S(2)}) %collective-permute-start) | collective-permute-done | bytes 393248 | tf_op jit(solution)/shard_map/ppermute | solution.py:376
  91.1 4.5 %all-gather.7.cloned.1.call-done.frames = bf16[2,16,192,128]{3,2,1,0:T(8,128)(2,1)} async-done(((bf16[2,2,192,128]{3,2,1,0:T(8,128)(2,1)}), bf16[2,16,192,128]{3,2,1,0:T(8,128)(2,1)}) %all-gather.7.cloned.1.call-update) | async-done | bytes 1572880 | tf_op jit(solution)/shard_map/all_gather | solution.py:339
  96.4 11.1 %shard_map.80 = (bf16[16,192,128]{2,1,0:T(8,128)(2,1)}, bf16[18,192,128]{2,1,0:T(8,128)(2,1)}) custom-call(s32[5,4]{1,0:T(8,128)} %add_add_fusion.flags, bf16[3,16,192,128]{3,2,1,0:T(8,128)(2,1)} %all-gather.5.cloned.1.call-done.caches.frames, bf16[18,192,128]{2,1,0:T(8,128)(2,1)} %get-tuple-element.34.a_p.a_pp, ...), custom_call_target="tpu_custom_call" | custom-call | tf_op jit(solution)/shard_map/pallas_call | solution.py:279
  107.5 7.5 %shard_map.81 = (bf16[8,192,128]{2,1,0:T(8,128)(2,1)}, bf16[18,192,128]{2,1,0:T(8,128)(2,1)}) custom-call(s32[5,4]{1,0:T(8,128)} %add_add_fusion.flags, bf16[2,16,192,128]{3,2,1,0:T(8,128)(2,1)} %bitcast.113, bf16[18,192,128]{2,1,0:T(8,128)(2,1)} %get-tuple-element.31.rest_0_.a_p.a_pp, bf16[18,192,128]{2,1,0:T(8,128)(2,1)} %broadcast_in_dim.8.a_p.a_pp, ...), custom_call_target="tpu_custom_call" | custom-call | tf_op jit(solution)/shard_map/pallas_call | solution.py:279
  115.0 3.4 %collective-permute-start.2 = (bf16[8,192,128]{2,1,0:T(8,128)(2,1)}, bf16[8,192,128]{2,1,0:T(8,128)(2,1)S(1)}, u32[]{:S(2)}, u32[]{:S(2)}) collective-permute-start(bf16[8,192,128]{2,1,0:T(8,128)(2,1)} %get-tuple-element.37), channel_id=1, source_target_pairs={{0,8},{8,16},{16,24},{1,9},{9,17},{17,25},{2,10},{10,18},{18,26},{... | collective-permute-start | bytes 1179656 | tf_op jit(solution)/shard_map/ppermute | solution.py:376
  118.4 7.3 %shard_map.82 = bf16[8,192,128]{2,1,0:T(8,128)(2,1)} custom-call(s32[5,4]{1,0:T(8,128)} %add_add_fusion.flags, bf16[2,16,192,128]{3,2,1,0:T(8,128)(2,1)} %bitcast.114, bf16[18,192,128]{2,1,0:T(8,128)(2,1)} %get-tuple-element.31.rest_0_.a_p.a_pp, bf16[18,192,128]{2,1,0:T(8,128)(2,1)} %broadcast_in_dim.8.a_p.a_pp, ...), custom_call_target="tpu_custom_call" | custom-call | tf_op jit(solution)/shard_map/pallas_call | solution.py:279
  125.7 3.6 %collective-permute-done.2.src_b = bf16[8,192,128]{2,1,0:T(8,128)(2,1)S(1)} collective-permute-done((bf16[8,192,128]{2,1,0:T(8,128)(2,1)}, bf16[8,192,128]{2,1,0:T(8,128)(2,1)S(1)}, u32[]{:S(2)}, u32[]{:S(2)}) %collective-permute-start.2) | collective-permute-done | bytes 393248 | tf_op jit(solution)/shard_map/ppermute | solution.py:376
  129.3 1.7 collective-permute-done.3.src_c
  131.8 11.1 %shard_map.83 = (bf16[16,192,128]{2,1,0:T(8,128)(2,1)}, bf16[18,192,128]{2,1,0:T(8,128)(2,1)}) custom-call(s32[5,4]{1,0:T(8,128)} %add_add_fusion.flags, bf16[3,16,192,128]{3,2,1,0:T(8,128)(2,1)} %all-gather.5.cloned.1.call-done.caches.frames, bf16[18,192,128]{2,1,0:T(8,128)(2,1)} %get-tuple-element.39.a_p.a_pp, ...), custom_call_target="tpu_custom_call" | custom-call | tf_op jit(solution)/shard_map/pallas_call | solution.py:279
  142.9 7.5 %shard_map.84 = (bf16[8,192,128]{2,1,0:T(8,128)(2,1)}, bf16[18,192,128]{2,1,0:T(8,128)(2,1)}) custom-call(s32[5,4]{1,0:T(8,128)} %add_add_fusion.flags, bf16[2,16,192,128]{3,2,1,0:T(8,128)(2,1)} %bitcast.115, bf16[18,192,128]{2,1,0:T(8,128)(2,1)} %get-tuple-element.36.rest_0_.a_p.a_pp, bf16[18,192,128]{2,1,0:T(8,128)(2,1)} %get-tuple-element.31.rest_0_.a_p.a_pp, ...), custom_call_target="tpu_custom_call" | custom-call | tf_op jit(solution)/shard_map/pallas_call | solution.py:279
  150.3 2.5 %collective-permute-start.4 = (bf16[8,192,128]{2,1,0:T(8,128)(2,1)}, bf16[8,192,128]{2,1,0:T(8,128)(2,1)S(1)}, u32[]{:S(2)}, u32[]{:S(2)}) collective-permute-start(bf16[8,192,128]{2,1,0:T(8,128)(2,1)} %get-tuple-element.42), channel_id=1, source_target_pairs={{0,8},{8,16},{16,24},{1,9},{9,17},{17,25},{2,10},{10,18},{18,26},{... | collective-permute-start | bytes 1179656 | tf_op jit(solution)/shard_map/ppermute | solution.py:376
  152.8 7.3 %shard_map.85 = bf16[8,192,128]{2,1,0:T(8,128)(2,1)} custom-call(s32[5,4]{1,0:T(8,128)} %add_add_fusion.flags, bf16[2,16,192,128]{3,2,1,0:T(8,128)(2,1)} %bitcast.116, bf16[18,192,128]{2,1,0:T(8,128)(2,1)} %get-tuple-element.36.rest_0_.a_p.a_pp, bf16[18,192,128]{2,1,0:T(8,128)(2,1)} %get-tuple-element.31.rest_0_.a_p.a_pp, ...), custom_call_target="tpu_custom_call" | custom-call | tf_op jit(solution)/shard_map/pallas_call | solution.py:279
  160.2 4.3 %collective-permute-done.4.src_b = bf16[8,192,128]{2,1,0:T(8,128)(2,1)S(1)} collective-permute-done((bf16[8,192,128]{2,1,0:T(8,128)(2,1)}, bf16[8,192,128]{2,1,0:T(8,128)(2,1)S(1)}, u32[]{:S(2)}, u32[]{:S(2)}) %collective-permute-start.4) | collective-permute-done | bytes 393248 | tf_op jit(solution)/shard_map/ppermute | solution.py:376
  164.5 1.7 collective-permute-done.5.src_c
  167.0 11.1 %shard_map.86 = (bf16[16,192,128]{2,1,0:T(8,128)(2,1)}, bf16[18,192,128]{2,1,0:T(8,128)(2,1)}) custom-call(s32[5,4]{1,0:T(8,128)} %add_add_fusion.flags, bf16[3,16,192,128]{3,2,1,0:T(8,128)(2,1)} %all-gather.5.cloned.1.call-done.caches.frames, bf16[18,192,128]{2,1,0:T(8,128)(2,1)} %get-tuple-element.44.a_p.a_pp, ...), custom_call_target="tpu_custom_call" | custom-call | tf_op jit(solution)/shard_map/pallas_call | solution.py:279
  178.1 7.5 %shard_map.87 = (bf16[8,192,128]{2,1,0:T(8,128)(2,1)}, bf16[18,192,128]{2,1,0:T(8,128)(2,1)}) custom-call(s32[5,4]{1,0:T(8,128)} %add_add_fusion.flags, bf16[2,16,192,128]{3,2,1,0:T(8,128)(2,1)} %bitcast.117, bf16[18,192,128]{2,1,0:T(8,128)(2,1)} %get-tuple-element.41.rest_0_.a_p.a_pp, bf16[18,192,128]{2,1,0:T(8,128)(2,1)} %get-tuple-element.36.rest_0_.a_p.a_pp, ...), custom_call_target="tpu_custom_call" | custom-call | tf_op jit(solution)/shard_map/pallas_call | solution.py:279
  185.6 1.9 collective-permute-start.6
  187.5 7.5 %shard_map.88 = bf16[8,192,128]{2,1,0:T(8,128)(2,1)} custom-call(s32[5,4]{1,0:T(8,128)} %add_add_fusion.flags, bf16[2,16,192,128]{3,2,1,0:T(8,128)(2,1)} %bitcast.118, bf16[18,192,128]{2,1,0:T(8,128)(2,1)} %get-tuple-element.41.rest_0_.a_p.a_pp, bf16[18,192,128]{2,1,0:T(8,128)(2,1)} %get-tuple-element.36.rest_0_.a_p.a_pp, ...), custom_call_target="tpu_custom_call" | custom-call | tf_op jit(solution)/shard_map/pallas_call | solution.py:279
  195.0 4.7 %collective-permute-done.6.src_b = bf16[8,192,128]{2,1,0:T(8,128)(2,1)S(1)} collective-permute-done((bf16[8,192,128]{2,1,0:T(8,128)(2,1)}, bf16[8,192,128]{2,1,0:T(8,128)(2,1)S(1)}, u32[]{:S(2)}, u32[]{:S(2)}) %collective-permute-start.6) | collective-permute-done | bytes 393248 | tf_op jit(solution)/shard_map/ppermute | solution.py:376
  199.8 1.3 select_bitcast_fusion.3
  202.2 11.2 %shard_map.89 = (bf16[16,192,128]{2,1,0:T(8,128)(2,1)}, bf16[18,192,128]{2,1,0:T(8,128)(2,1)}) custom-call(s32[5,4]{1,0:T(8,128)} %add_add_fusion.flags, bf16[3,16,192,128]{3,2,1,0:T(8,128)(2,1)} %all-gather.5.cloned.1.call-done.caches.frames, bf16[18,192,128]{2,1,0:T(8,128)(2,1)} %get-tuple-element.53.a_p, ...), custom_call_target="tpu_custom_call" | custom-call | tf_op jit(solution)/shard_map/pallas_call | solution.py:279
  213.4 1.1 fusion.7
  214.6 7.5 %shard_map.90 = (bf16[8,192,128]{2,1,0:T(8,128)(2,1)}, bf16[18,192,128]{2,1,0:T(8,128)(2,1)}) custom-call(s32[5,4]{1,0:T(8,128)} %add_add_fusion.flags, bf16[2,16,192,128]{3,2,1,0:T(8,128)(2,1)} %bitcast.119, bf16[18,192,128]{2,1,0:T(8,128)(2,1)} %get-tuple-element.47.rest_0_.a_p, bf16[18,192,128]{2,1,0:T(8,128)(2,1)} %get-tuple-element.41.rest_0_.a_p.a_pp, ...), custom_call_target="tpu_custom_call" | custom-call | tf_op jit(solution)/shard_map/pallas_call | solution.py:279
  222.0 1.1 fusion.1
  223.3 1.2 copy.64
  224.4 7.1 %shard_map.91 = bf16[8,192,128]{2,1,0:T(8,128)(2,1)} custom-call(s32[5,4]{1,0:T(8,128)} %add_add_fusion.flags, bf16[2,16,192,128]{3,2,1,0:T(8,128)(2,1)} %bitcast.120, bf16[18,192,128]{2,1,0:T(8,128)(2,1)} %get-tuple-element.47.rest_0_.a_p, bf16[18,192,128]{2,1,0:T(8,128)(2,1)} %get-tuple-element.41.rest_0_.a_p.a_pp, ...), custom_call_target="tpu_custom_call" | custom-call | tf_op jit(solution)/shard_map/pallas_call | solution.py:279
  231.6 1.2 select_bitcast_fusion.2
  232.8 0.9 copy.63
  (62 shorter events, 9.4 us)
Async XLA Ops:
  7.2 35.9 %all-gather.5.cloned.1.call-start = ((), (), s32[]{:S(2)}) async-start(), calls=%async_computation | async-start | bytes 2654208 | tf_op jit(solution)/shard_map/all_gather | solution.py:334
  10.0 59.4 %all-gather.9.cloned.1.call-start = ((), (), s32[]{:S(2)}) async-start(), calls=%async_computation.2 | async-start | bytes 1769472 | tf_op jit(solution)/shard_map/all_gather | solution.py:335
  10.8 84.9 %all-gather.7.cloned.1.call-start = ((), (), s32[]{:S(2)}) async-start(), calls=%async_computation.1 | async-start | bytes 1769472 | tf_op jit(solution)/shard_map/all_gather | solution.py:339
  19.7 4.6 %copy-start.10 = (f32[1,2,192]{2,1,0:T(2,128)S(1)}, f32[1,2,192]{2,1,0:T(2,128)}, u32[]{:S(2)}) copy-start(f32[1,2,192]{2,1,0:T(2,128)} %param.9) | copy-start | bytes 4612
  19.7 5.4 %copy-start.11 = (f32[1,2,192]{2,1,0:T(2,128)S(1)}, f32[1,2,192]{2,1,0:T(2,128)}, u32[]{:S(2)}) copy-start(f32[1,2,192]{2,1,0:T(2,128)} %param.10) | copy-start | bytes 4612
  19.8 6.1 %copy-start.12 = (f32[1,2,192]{2,1,0:T(2,128)S(1)}, f32[1,2,192]{2,1,0:T(2,128)}, u32[]{:S(2)}) copy-start(f32[1,2,192]{2,1,0:T(2,128)} %param.11) | copy-start | bytes 4612
  30.7 6.6 %copy-start.13 = (s32[4]{0:T(128)S(1)}, s32[4]{0:T(128)}, u32[]{:S(2)}) copy-start(s32[4]{0:T(128)} %pad.15.clone) | copy-start | bytes 52
  76.9 14.3 %collective-permute-start = (bf16[8,192,128]{2,1,0:T(8,128)(2,1)}, bf16[8,192,128]{2,1,0:T(8,128)(2,1)S(1)}, u32[]{:S(2)}, u32[]{:S(2)}) collective-permute-start(bf16[8,192,128]{2,1,0:T(8,128)(2,1)} %get-tuple-element.32), channel_id=1, source_target_pairs={{0,8},{8,16},{16,24},{1,9},{9,17},{17,25},{2,10},{10,18},{18,26},{... | collective-permute-start | bytes 1179656 | tf_op jit(solution)/shard_map/ppermute | solution.py:376
  91.1 4.5 %copy-start.3 = (bf16[8,192,128]{2,1,0:T(8,128)(2,1)}, bf16[8,192,128]{2,1,0:T(8,128)(2,1)S(1)}, u32[]{:S(2)}) copy-start(bf16[8,192,128]{2,1,0:T(8,128)(2,1)S(1)} %collective-permute-done.src_b) | copy-start | bytes 1179652
  91.1 4.5 %collective-permute-start.1 = (bf16[8,192,128]{2,1,0:T(8,128)(2,1)S(1)}, bf16[8,192,128]{2,1,0:T(8,128)(2,1)S(1)}, u32[]{:S(2)}, u32[]{:S(2)}) collective-permute-start(bf16[8,192,128]{2,1,0:T(8,128)(2,1)S(1)} %collective-permute-done.src_b), channel_id=1, source_target_pairs={{0,1},{1,0},{2,3},{3,2},{4,5},{5,4},{6,7},{7,6},{8,9},{9,8},{10,11... | collective-permute-start | bytes 1179656 | tf_op jit(solution)/shard_map/ppermute | solution.py:378
  95.7 0.8 copy-start.6
  115.0 14.3 %collective-permute-start.2 = (bf16[8,192,128]{2,1,0:T(8,128)(2,1)}, bf16[8,192,128]{2,1,0:T(8,128)(2,1)S(1)}, u32[]{:S(2)}, u32[]{:S(2)}) collective-permute-start(bf16[8,192,128]{2,1,0:T(8,128)(2,1)} %get-tuple-element.37), channel_id=1, source_target_pairs={{0,8},{8,16},{16,24},{1,9},{9,17},{17,25},{2,10},{10,18},{18,26},{... | collective-permute-start | bytes 1179656 | tf_op jit(solution)/shard_map/ppermute | solution.py:376
  129.3 1.7 copy-start.4
  129.3 1.7 collective-permute-start.3
  131.0 0.8 copy-start.7
  150.3 14.2 %collective-permute-start.4 = (bf16[8,192,128]{2,1,0:T(8,128)(2,1)}, bf16[8,192,128]{2,1,0:T(8,128)(2,1)S(1)}, u32[]{:S(2)}, u32[]{:S(2)}) collective-permute-start(bf16[8,192,128]{2,1,0:T(8,128)(2,1)} %get-tuple-element.42), channel_id=1, source_target_pairs={{0,8},{8,16},{16,24},{1,9},{9,17},{17,25},{2,10},{10,18},{18,26},{... | collective-permute-start | bytes 1179656 | tf_op jit(solution)/shard_map/ppermute | solution.py:376
  164.5 1.7 copy-start.5
  164.5 1.7 collective-permute-start.5
  166.2 0.7 copy-start.8
  185.6 14.2 %collective-permute-start.6 = (bf16[8,192,128]{2,1,0:T(8,128)(2,1)}, bf16[8,192,128]{2,1,0:T(8,128)(2,1)S(1)}, u32[]{:S(2)}, u32[]{:S(2)}) collective-permute-start(bf16[8,192,128]{2,1,0:T(8,128)(2,1)} %get-tuple-element.46), channel_id=1, source_target_pairs={{0,8},{8,16},{16,24},{1,9},{9,17},{17,25},{2,10},{10,18},{18,26},{... | collective-permute-start | bytes 1179656 | tf_op jit(solution)/shard_map/ppermute | solution.py:376
  187.5 12.2 %copy-start = (bf16[1,2,16,192,128]{4,3,2,1,0:T(8,128)(2,1)S(1)}, bf16[1,2,16,192,128]{4,3,2,1,0:T(8,128)(2,1)}, u32[]{:S(2)}) copy-start(bf16[1,2,16,192,128]{4,3,2,1,0:T(8,128)(2,1)} %all-gather.9.cloned.1.call-done) | copy-start | bytes 4718596
  195.0 4.8 %copy-start.9 = (bf16[8,192,128]{2,1,0:T(8,128)(2,1)S(1)}, bf16[8,192,128]{2,1,0:T(8,128)(2,1)}, u32[]{:S(2)}) copy-start(bf16[8,192,128]{2,1,0:T(8,128)(2,1)} %shard_map.82) | copy-start | bytes 1179652
  199.7 1.7 copy-start.1
  199.7 1.7 collective-permute-start.7
  201.5 0.7 copy-start.2
  202.2 11.2 %slice-start = ((bf16[3,16,192,128]{3,2,1,0:T(8,128)(2,1)}), bf16[1,16,192,128]{3,2,1,0:T(8,128)(2,1)S(1)}, s32[]{:S(2)}) async-start(bf16[3,16,192,128]{3,2,1,0:T(8,128)(2,1)} %all-gather.5.cloned.1.call-done.caches.frames), calls=%async_computation.3 | async-start | bytes 1572864 | tf_op jit(solution)/shard_map/slice | solution.py:382
Sparse Core Ops, SparseCore 0:
  10.2 32.8 all-gather.4
  45.2 24.1 all-gather.8
  71.0 24.5 all-gather.6

commit v2 on v1

--- a/solution.py
+++ b/solution.py
@@ -249,6 +249,9 @@
     finish(history_copies, 2)
     if kind == "first":
         conv_span(x0, x1, act, taps, bias, None, out, 0, span)
+    elif kind == "all":
+        finish(source_copies, 0)
+        conv_span(x0, x1, act, taps, bias, rawbuf, out, 0, span)
     else:
         finish(source_copies, 0)
         base = core * half if kind == "lead" else (1 - core) * half
@@ -269,7 +272,7 @@
     if own is not None:
         args.append(own)
         specs.append(vmem)
-    rows_out = span if kind == "first" else span // 2
+    rows_out = span if kind in ("first", "all") else span // 2
     result = jax.ShapeDtypeStruct((rows_out, outputs, columns), jnp.bfloat16)
     padded = jax.ShapeDtypeStruct((span + 2, channels, columns), jnp.bfloat16)
     shapes = result if kind == "tail" else (result, padded)
@@ -370,8 +373,13 @@
             taps[0], conv_bias[0, 0], (norm_gain[0, 0], norm_shift[0, 0]), "first",
         )
         second = (flags, tick_no, cache_of[1][0], cache_of[1][1], recents[1], *common, taps[1], conv_bias[0, 1])
-        lead, second_in = fused_conv(*second, (norm_gain[0, 1], norm_shift[0, 1]), "lead", hidden)
-        tail = fused_conv(*second, (norm_gain[0, 1], norm_shift[0, 1]), "tail", second_in)
+        if tick_no + 1 == tick_count:
+            whole_out, second_in = fused_conv(*second, (norm_gain[0, 1], norm_shift[0, 1]), "all", hidden)
+            lead = lax.dynamic_slice_in_dim(whole_out, core * half, half, axis=0)
+            tail = lax.dynamic_slice_in_dim(whole_out, (1 - core) * half, half, axis=0)
+        else:
+            lead, second_in = fused_conv(*second, (norm_gain[0, 1], norm_shift[0, 1]), "lead", hidden)
+            tail = fused_conv(*second, (norm_gain[0, 1], norm_shift[0, 1]), "tail", second_in)
         if tick_no + 1 < tick_count:
             got = lax.ppermute(lead, "phase", forward)
             got, tail = lax.optimization_barrier((got, tail))

time: 245 us -> 241 us (0.984)
  Pallas kernels: 130 us -> 126 us
    pallas_call x15 -> x14, Pallas kernels: 130 us -> 126 us  [fused_conv(): pl.pallas_call(body, out_shape=shapes, in_specs=specs, out_specs=vmem if...]
  transfers between devices with their start and end apart: 11 -> 11, of which waited for: 10 -> 9; matrix products, arithmetic and copies ran while one was open for 13% -> 14% of each run, Pallas kernels for 20% -> 21%
where the time goes in v2:
time: 241 us; the launch traced here: 237 us
  Pallas kernels  126 us (52%)
  waiting for transfers between devices  40.5 us (17%)
  local copies, waits for them, and re-layouts  36.4 us (15%)
  between operations  14.4 us (6%)
  starting transfers between devices  11.3 us (5%)
  other arithmetic  8.39 us (3%)
    pallas_call x14, Pallas kernels, fused_conv(): pl.pallas_call(body, out_shape=shapes, in_specs=specs, out_specs=vmem if...  126 us
    ppermute x4, waiting for transfers between devices, shards_whole(): got = lax.ppermute(lead, 'phase', forward)  15.9 us
    all_gather x1, waiting for transfers between devices, shards_whole(): second_cache = lax.all_gather(cache_t[1], 'rows', axis=1, tiled=True)  13 us
    ppermute x4, starting transfers between devices, shards_whole(): got = lax.ppermute(lead, 'phase', forward)  11.1 us
    transpose x3, local copies, waits for them, and re-layouts, arrange_taps(): jnp.transpose(weight, (2, 3, 0, 1, 4)).reshape(3 * outputs, 9 * channels)  11 us
    reshape x2, local copies, waits for them, and re-layouts, arrange_taps(): jnp.transpose(weight, (2, 3, 0, 1, 4)).reshape(3 * outputs, 9 * channels)  8.81 us
    unnamed x32, local copies, waits for them, and re-layouts  7.07 us
  transfers between devices with their start and end apart: 11, of which 9 were waited for; matrix products, arithmetic and copies ran while one was open for 14% of the time, Pallas kernels for 21%

profile of v2, /device:TPU:4, one launch (start us, length us, event | category | flops | bytes accessed | tf_op | source)
XLA Modules:
  0.0 236.8 jit_solution(10587823881601454173)
XLA Ops:
  7.2 1.0 copy.64
  8.3 1.0 copy.65
  12.8 4.7 %slice_bitcast_fusion = (bf16[3,192,3,3,192]{4,1,0,3,2:T(8,128)(2,1)S(1)}, bf16[3,192,3,3,192]{4,1,0,3,2:T(8,128)(2,1)}) fusion(bf16[1,2,3,3,3,192,192]{6,5,4,3,2,1,0:T(8,128)(2,1)} %param.8), kind=kLoop, calls=%fused_computation | loop fusion | bytes 7962624 | tf_op jit(solution)/shard_map/transpose | solution.py:77
  17.5 2.3 copy.17
  19.8 4.6 %reshape.59.taps = bf16[576,1728]{1,0:T(8,128)(2,1)} reshape(bf16[3,192,3,3,192]{4,3,2,1,0:T(4,128)(2,1)S(1)} %copy.17) | data formatting | bytes 3981312 | tf_op jit(solution)/shard_map/reshape | solution.py:77
  24.4 0.8 copy.18.bias
  25.2 0.8 copy.19.gain
  26.7 4.0 %copy.16 = bf16[3,192,3,3,192]{4,3,2,1,0:T(4,128)(2,1)S(1)} copy(bf16[3,192,3,3,192]{4,1,0,3,2:T(8,128)(2,1)} %get-tuple-element.63) | data formatting | bytes 3981312 | tf_op jit(solution)/shard_map/transpose | solution.py:77
  30.8 4.2 %reshape.58.taps = bf16[576,1728]{1,0:T(8,128)(2,1)} reshape(bf16[3,192,3,3,192]{4,3,2,1,0:T(4,128)(2,1)S(1)} %copy.16) | data formatting | bytes 3981312 | tf_op jit(solution)/shard_map/reshape | solution.py:77
  35.0 0.8 copy.21.bias
  37.3 1.3 add_add_fusion.flags
  38.6 0.8 compare_convert_fusion.member
  39.4 3.7 %all-gather.5.cloned.1.call-done.caches.frames = bf16[3,16,192,128]{3,2,1,0:T(8,128)(2,1)} async-done(((bf16[3,2,192,128]{3,2,1,0:T(8,128)(2,1)}), bf16[3,16,192,128]{3,2,1,0:T(8,128)(2,1)}) %all-gather.5.cloned.1.call-update) | async-done | bytes 2359312 | tf_op jit(solution)/shard_map/all_gather | solution.py:337
  43.0 1.2 broadcast_in_dim.8.a_p.a_pp
  44.2 0.8 broadcast_in_dim.9.src_b.src_c
  45.0 11.4 %shard_map.77 = (bf16[16,192,128]{2,1,0:T(8,128)(2,1)}, bf16[18,192,128]{2,1,0:T(8,128)(2,1)}) custom-call(s32[5,4]{1,0:T(8,128)} %add_add_fusion.flags, bf16[3,16,192,128]{3,2,1,0:T(8,128)(2,1)} %all-gather.5.cloned.1.call-done.caches.frames, bf16[18,192,128]{2,1,0:T(8,128)(2,1)} %broadcast_in_dim.8.a_p.a_pp, ...), custom_call_target="tpu_custom_call" | custom-call | tf_op jit(solution)/shard_map/pallas_call | solution.py:282
  56.4 13.0 %all-gather.9.cloned.1.call-done = bf16[1,2,16,192,128]{4,3,2,1,0:T(8,128)(2,1)} async-done(((bf16[1,2,2,192,128]{4,3,2,1,0:T(8,128)(2,1)}), bf16[1,2,16,192,128]{4,3,2,1,0:T(8,128)(2,1)}) %all-gather.9.cloned.1.call-update) | async-done | bytes 1572880 | tf_op jit(solution)/shard_map/all_gather | solution.py:338
  69.4 7.5 %shard_map.78 = (bf16[8,192,128]{2,1,0:T(8,128)(2,1)}, bf16[18,192,128]{2,1,0:T(8,128)(2,1)}) custom-call(s32[5,4]{1,0:T(8,128)} %add_add_fusion.flags, bf16[2,16,192,128]{3,2,1,0:T(8,128)(2,1)} %bitcast.111, bf16[18,192,128]{2,1,0:T(8,128)(2,1)} %broadcast_in_dim.8.a_p.a_pp, bf16[18,192,128]{2,1,0:T(8,128)(2,1)} %broadcast_in_dim.8.a_p.a_pp, ...), custom_call_target="tpu_custom_call" | custom-call | tf_op jit(solution)/shard_map/pallas_call | solution.py:282
  76.9 3.4 %collective-permute-start = (bf16[8,192,128]{2,1,0:T(8,128)(2,1)}, bf16[8,192,128]{2,1,0:T(8,128)(2,1)S(1)}, u32[]{:S(2)}, u32[]{:S(2)}) collective-permute-start(bf16[8,192,128]{2,1,0:T(8,128)(2,1)} %get-tuple-element.32), channel_id=1, source_target_pairs={{0,8},{8,16},{16,24},{1,9},{9,17},{17,25},{2,10},{10,18},{18,26},{... | collective-permute-start | bytes 1179656 | tf_op jit(solution)/shard_map/ppermute | solution.py:384
  80.3 7.7 %shard_map.79 = bf16[8,192,128]{2,1,0:T(8,128)(2,1)} custom-call(s32[5,4]{1,0:T(8,128)} %add_add_fusion.flags, bf16[2,16,192,128]{3,2,1,0:T(8,128)(2,1)} %bitcast.112, bf16[18,192,128]{2,1,0:T(8,128)(2,1)} %broadcast_in_dim.8.a_p.a_pp, bf16[18,192,128]{2,1,0:T(8,128)(2,1)} %broadcast_in_dim.8.a_p.a_pp, ...), custom_call_target="tpu_custom_call" | custom-call | tf_op jit(solution)/shard_map/pallas_call | solution.py:282
  88.0 3.2 %collective-permute-done.src_b = bf16[8,192,128]{2,1,0:T(8,128)(2,1)S(1)} collective-permute-done((bf16[8,192,128]{2,1,0:T(8,128)(2,1)}, bf16[8,192,128]{2,1,0:T(8,128)(2,1)S(1)}, u32[]{:S(2)}, u32[]{:S(2)}) %collective-permute-start) | collective-permute-done | bytes 393248 | tf_op jit(solution)/shard_map/ppermute | solution.py:384
  91.2 4.5 %all-gather.7.cloned.1.call-done.frames = bf16[2,16,192,128]{3,2,1,0:T(8,128)(2,1)} async-done(((bf16[2,2,192,128]{3,2,1,0:T(8,128)(2,1)}), bf16[2,16,192,128]{3,2,1,0:T(8,128)(2,1)}) %all-gather.7.cloned.1.call-update) | async-done | bytes 1572880 | tf_op jit(solution)/shard_map/all_gather | solution.py:342
  96.4 11.1 %shard_map.80 = (bf16[16,192,128]{2,1,0:T(8,128)(2,1)}, bf16[18,192,128]{2,1,0:T(8,128)(2,1)}) custom-call(s32[5,4]{1,0:T(8,128)} %add_add_fusion.flags, bf16[3,16,192,128]{3,2,1,0:T(8,128)(2,1)} %all-gather.5.cloned.1.call-done.caches.frames, bf16[18,192,128]{2,1,0:T(8,128)(2,1)} %get-tuple-element.34.a_p.a_pp, ...), custom_call_target="tpu_custom_call" | custom-call | tf_op jit(solution)/shard_map/pallas_call | solution.py:282
  107.5 7.5 %shard_map.81 = (bf16[8,192,128]{2,1,0:T(8,128)(2,1)}, bf16[18,192,128]{2,1,0:T(8,128)(2,1)}) custom-call(s32[5,4]{1,0:T(8,128)} %add_add_fusion.flags, bf16[2,16,192,128]{3,2,1,0:T(8,128)(2,1)} %bitcast.113, bf16[18,192,128]{2,1,0:T(8,128)(2,1)} %get-tuple-element.31.rest_0_.a_p.a_pp, bf16[18,192,128]{2,1,0:T(8,128)(2,1)} %broadcast_in_dim.8.a_p.a_pp, ...), custom_call_target="tpu_custom_call" | custom-call | tf_op jit(solution)/shard_map/pallas_call | solution.py:282
  115.0 3.4 %collective-permute-start.2 = (bf16[8,192,128]{2,1,0:T(8,128)(2,1)}, bf16[8,192,128]{2,1,0:T(8,128)(2,1)S(1)}, u32[]{:S(2)}, u32[]{:S(2)}) collective-permute-start(bf16[8,192,128]{2,1,0:T(8,128)(2,1)} %get-tuple-element.37), channel_id=1, source_target_pairs={{0,8},{8,16},{16,24},{1,9},{9,17},{17,25},{2,10},{10,18},{18,26},{... | collective-permute-start | bytes 1179656 | tf_op jit(solution)/shard_map/ppermute | solution.py:384
  118.4 7.3 %shard_map.82 = bf16[8,192,128]{2,1,0:T(8,128)(2,1)} custom-call(s32[5,4]{1,0:T(8,128)} %add_add_fusion.flags, bf16[2,16,192,128]{3,2,1,0:T(8,128)(2,1)} %bitcast.114, bf16[18,192,128]{2,1,0:T(8,128)(2,1)} %get-tuple-element.31.rest_0_.a_p.a_pp, bf16[18,192,128]{2,1,0:T(8,128)(2,1)} %broadcast_in_dim.8.a_p.a_pp, ...), custom_call_target="tpu_custom_call" | custom-call | tf_op jit(solution)/shard_map/pallas_call | solution.py:282
  125.7 3.6 %collective-permute-done.2.src_b = bf16[8,192,128]{2,1,0:T(8,128)(2,1)S(1)} collective-permute-done((bf16[8,192,128]{2,1,0:T(8,128)(2,1)}, bf16[8,192,128]{2,1,0:T(8,128)(2,1)S(1)}, u32[]{:S(2)}, u32[]{:S(2)}) %collective-permute-start.2) | collective-permute-done | bytes 393248 | tf_op jit(solution)/shard_map/ppermute | solution.py:384
  129.3 1.7 collective-permute-done.3.src_c
  131.7 11.1 %shard_map.83 = (bf16[16,192,128]{2,1,0:T(8,128)(2,1)}, bf16[18,192,128]{2,1,0:T(8,128)(2,1)}) custom-call(s32[5,4]{1,0:T(8,128)} %add_add_fusion.flags, bf16[3,16,192,128]{3,2,1,0:T(8,128)(2,1)} %all-gather.5.cloned.1.call-done.caches.frames, bf16[18,192,128]{2,1,0:T(8,128)(2,1)} %get-tuple-element.39.a_p.a_pp, ...), custom_call_target="tpu_custom_call" | custom-call | tf_op jit(solution)/shard_map/pallas_call | solution.py:282
  142.9 7.5 %shard_map.84 = (bf16[8,192,128]{2,1,0:T(8,128)(2,1)}, bf16[18,192,128]{2,1,0:T(8,128)(2,1)}) custom-call(s32[5,4]{1,0:T(8,128)} %add_add_fusion.flags, bf16[2,16,192,128]{3,2,1,0:T(8,128)(2,1)} %bitcast.115, bf16[18,192,128]{2,1,0:T(8,128)(2,1)} %get-tuple-element.36.rest_0_.a_p.a_pp, bf16[18,192,128]{2,1,0:T(8,128)(2,1)} %get-tuple-element.31.rest_0_.a_p.a_pp, ...), custom_call_target="tpu_custom_call" | custom-call | tf_op jit(solution)/shard_map/pallas_call | solution.py:282
  150.3 2.5 %collective-permute-start.4 = (bf16[8,192,128]{2,1,0:T(8,128)(2,1)}, bf16[8,192,128]{2,1,0:T(8,128)(2,1)S(1)}, u32[]{:S(2)}, u32[]{:S(2)}) collective-permute-start(bf16[8,192,128]{2,1,0:T(8,128)(2,1)} %get-tuple-element.42), channel_id=1, source_target_pairs={{0,8},{8,16},{16,24},{1,9},{9,17},{17,25},{2,10},{10,18},{18,26},{... | collective-permute-start | bytes 1179656 | tf_op jit(solution)/shard_map/ppermute | solution.py:384
  152.8 7.3 %shard_map.85 = bf16[8,192,128]{2,1,0:T(8,128)(2,1)} custom-call(s32[5,4]{1,0:T(8,128)} %add_add_fusion.flags, bf16[2,16,192,128]{3,2,1,0:T(8,128)(2,1)} %bitcast.116, bf16[18,192,128]{2,1,0:T(8,128)(2,1)} %get-tuple-element.36.rest_0_.a_p.a_pp, bf16[18,192,128]{2,1,0:T(8,128)(2,1)} %get-tuple-element.31.rest_0_.a_p.a_pp, ...), custom_call_target="tpu_custom_call" | custom-call | tf_op jit(solution)/shard_map/pallas_call | solution.py:282
  160.1 4.4 %collective-permute-done.4.src_b = bf16[8,192,128]{2,1,0:T(8,128)(2,1)S(1)} collective-permute-done((bf16[8,192,128]{2,1,0:T(8,128)(2,1)}, bf16[8,192,128]{2,1,0:T(8,128)(2,1)S(1)}, u32[]{:S(2)}, u32[]{:S(2)}) %collective-permute-start.4) | collective-permute-done | bytes 393248 | tf_op jit(solution)/shard_map/ppermute | solution.py:384
  164.5 1.7 collective-permute-done.5.src_c
  167.0 11.1 %shard_map.86 = (bf16[16,192,128]{2,1,0:T(8,128)(2,1)}, bf16[18,192,128]{2,1,0:T(8,128)(2,1)}) custom-call(s32[5,4]{1,0:T(8,128)} %add_add_fusion.flags, bf16[3,16,192,128]{3,2,1,0:T(8,128)(2,1)} %all-gather.5.cloned.1.call-done.caches.frames, bf16[18,192,128]{2,1,0:T(8,128)(2,1)} %get-tuple-element.44.a_p.a_pp, ...), custom_call_target="tpu_custom_call" | custom-call | tf_op jit(solution)/shard_map/pallas_call | solution.py:282
  178.1 7.5 %shard_map.87 = (bf16[8,192,128]{2,1,0:T(8,128)(2,1)}, bf16[18,192,128]{2,1,0:T(8,128)(2,1)}) custom-call(s32[5,4]{1,0:T(8,128)} %add_add_fusion.flags, bf16[2,16,192,128]{3,2,1,0:T(8,128)(2,1)} %bitcast.117, bf16[18,192,128]{2,1,0:T(8,128)(2,1)} %get-tuple-element.41.rest_0_.a_p.a_pp, bf16[18,192,128]{2,1,0:T(8,128)(2,1)} %get-tuple-element.36.rest_0_.a_p.a_pp, ...), custom_call_target="tpu_custom_call" | custom-call | tf_op jit(solution)/shard_map/pallas_call | solution.py:282
  185.6 1.9 collective-permute-start.6
  187.5 7.4 %shard_map.88 = bf16[8,192,128]{2,1,0:T(8,128)(2,1)} custom-call(s32[5,4]{1,0:T(8,128)} %add_add_fusion.flags, bf16[2,16,192,128]{3,2,1,0:T(8,128)(2,1)} %bitcast.118, bf16[18,192,128]{2,1,0:T(8,128)(2,1)} %get-tuple-element.41.rest_0_.a_p.a_pp, bf16[18,192,128]{2,1,0:T(8,128)(2,1)} %get-tuple-element.36.rest_0_.a_p.a_pp, ...), custom_call_target="tpu_custom_call" | custom-call | tf_op jit(solution)/shard_map/pallas_call | solution.py:282
  195.0 4.8 %collective-permute-done.6.src_b = bf16[8,192,128]{2,1,0:T(8,128)(2,1)S(1)} collective-permute-done((bf16[8,192,128]{2,1,0:T(8,128)(2,1)}, bf16[8,192,128]{2,1,0:T(8,128)(2,1)S(1)}, u32[]{:S(2)}, u32[]{:S(2)}) %collective-permute-start.6) | collective-permute-done | bytes 393248 | tf_op jit(solution)/shard_map/ppermute | solution.py:384
  199.7 1.0 slice.52
  200.7 1.2 select_bitcast_fusion.3
  202.7 11.2 %shard_map.89 = (bf16[16,192,128]{2,1,0:T(8,128)(2,1)}, bf16[18,192,128]{2,1,0:T(8,128)(2,1)}) custom-call(s32[5,4]{1,0:T(8,128)} %add_add_fusion.flags, bf16[3,16,192,128]{3,2,1,0:T(8,128)(2,1)} %all-gather.5.cloned.1.call-done.caches.frames, bf16[18,192,128]{2,1,0:T(8,128)(2,1)} %get-tuple-element.53.a_p, ...), custom_call_target="tpu_custom_call" | custom-call | tf_op jit(solution)/shard_map/pallas_call | solution.py:282
  213.9 1.1 fusion.7
  215.1 10.3 %shard_map.90 = (bf16[16,192,128]{2,1,0:T(8,128)(2,1)}, bf16[18,192,128]{2,1,0:T(8,128)(2,1)}) custom-call(s32[5,4]{1,0:T(8,128)} %add_add_fusion.flags, bf16[2,16,192,128]{3,2,1,0:T(8,128)(2,1)} %bitcast.119, bf16[18,192,128]{2,1,0:T(8,128)(2,1)} %get-tuple-element.47.rest_0_.a_p, bf16[18,192,128]{2,1,0:T(8,128)(2,1)} %get-tuple-element.41.rest_0_.a_p.a_pp, ...), custom_call_target="tpu_custom_call" | custom-call | tf_op jit(solution)/shard_map/pallas_call | solution.py:282
  225.4 1.2 fusion.1
  226.7 1.2 copy.61
  227.8 1.2 select_bitcast_fusion.2
  229.1 0.9 copy.60
  (61 shorter events, 9.1 us)
Async XLA Ops:
  7.2 35.9 %all-gather.5.cloned.1.call-start = ((), (), s32[]{:S(2)}) async-start(), calls=%async_computation | async-start | bytes 2654208 | tf_op jit(solution)/shard_map/all_gather | solution.py:337
  10.0 59.4 %all-gather.9.cloned.1.call-start = ((), (), s32[]{:S(2)}) async-start(), calls=%async_computation.2 | async-start | bytes 1769472 | tf_op jit(solution)/shard_map/all_gather | solution.py:338
  10.8 84.9 %all-gather.7.cloned.1.call-start = ((), (), s32[]{:S(2)}) async-start(), calls=%async_computation.1 | async-start | bytes 1769472 | tf_op jit(solution)/shard_map/all_gather | solution.py:342
  19.8 4.6 %copy-start.10 = (f32[1,2,192]{2,1,0:T(2,128)S(1)}, f32[1,2,192]{2,1,0:T(2,128)}, u32[]{:S(2)}) copy-start(f32[1,2,192]{2,1,0:T(2,128)} %param.9) | copy-start | bytes 4612
  19.8 5.4 %copy-start.11 = (f32[1,2,192]{2,1,0:T(2,128)S(1)}, f32[1,2,192]{2,1,0:T(2,128)}, u32[]{:S(2)}) copy-start(f32[1,2,192]{2,1,0:T(2,128)} %param.10) | copy-start | bytes 4612
  19.8 6.1 %copy-start.12 = (f32[1,2,192]{2,1,0:T(2,128)S(1)}, f32[1,2,192]{2,1,0:T(2,128)}, u32[]{:S(2)}) copy-start(f32[1,2,192]{2,1,0:T(2,128)} %param.11) | copy-start | bytes 4612
  30.7 6.6 %copy-start.13 = (s32[4]{0:T(128)S(1)}, s32[4]{0:T(128)}, u32[]{:S(2)}) copy-start(s32[4]{0:T(128)} %pad.15.clone) | copy-start | bytes 52
  76.9 14.3 %collective-permute-start = (bf16[8,192,128]{2,1,0:T(8,128)(2,1)}, bf16[8,192,128]{2,1,0:T(8,128)(2,1)S(1)}, u32[]{:S(2)}, u32[]{:S(2)}) collective-permute-start(bf16[8,192,128]{2,1,0:T(8,128)(2,1)} %get-tuple-element.32), channel_id=1, source_target_pairs={{0,8},{8,16},{16,24},{1,9},{9,17},{17,25},{2,10},{10,18},{18,26},{... | collective-permute-start | bytes 1179656 | tf_op jit(solution)/shard_map/ppermute | solution.py:384
  91.2 4.5 %copy-start.1 = (bf16[8,192,128]{2,1,0:T(8,128)(2,1)}, bf16[8,192,128]{2,1,0:T(8,128)(2,1)S(1)}, u32[]{:S(2)}) copy-start(bf16[8,192,128]{2,1,0:T(8,128)(2,1)S(1)} %collective-permute-done.src_b) | copy-start | bytes 1179652
  91.2 4.5 %collective-permute-start.1 = (bf16[8,192,128]{2,1,0:T(8,128)(2,1)S(1)}, bf16[8,192,128]{2,1,0:T(8,128)(2,1)S(1)}, u32[]{:S(2)}, u32[]{:S(2)}) collective-permute-start(bf16[8,192,128]{2,1,0:T(8,128)(2,1)S(1)} %collective-permute-done.src_b), channel_id=1, source_target_pairs={{0,1},{1,0},{2,3},{3,2},{4,5},{5,4},{6,7},{7,6},{8,9},{9,8},{10,11... | collective-permute-start | bytes 1179656 | tf_op jit(solution)/shard_map/ppermute | solution.py:386
  95.7 0.8 copy-start.4
  115.0 14.3 %collective-permute-start.2 = (bf16[8,192,128]{2,1,0:T(8,128)(2,1)}, bf16[8,192,128]{2,1,0:T(8,128)(2,1)S(1)}, u32[]{:S(2)}, u32[]{:S(2)}) collective-permute-start(bf16[8,192,128]{2,1,0:T(8,128)(2,1)} %get-tuple-element.37), channel_id=1, source_target_pairs={{0,8},{8,16},{16,24},{1,9},{9,17},{17,25},{2,10},{10,18},{18,26},{... | collective-permute-start | bytes 1179656 | tf_op jit(solution)/shard_map/ppermute | solution.py:384
  129.3 1.7 copy-start.2
  129.3 1.7 collective-permute-start.3
  131.0 0.7 copy-start.5
  150.3 14.2 %collective-permute-start.4 = (bf16[8,192,128]{2,1,0:T(8,128)(2,1)}, bf16[8,192,128]{2,1,0:T(8,128)(2,1)S(1)}, u32[]{:S(2)}, u32[]{:S(2)}) collective-permute-start(bf16[8,192,128]{2,1,0:T(8,128)(2,1)} %get-tuple-element.42), channel_id=1, source_target_pairs={{0,8},{8,16},{16,24},{1,9},{9,17},{17,25},{2,10},{10,18},{18,26},{... | collective-permute-start | bytes 1179656 | tf_op jit(solution)/shard_map/ppermute | solution.py:384
  164.5 1.7 copy-start.3
  164.5 1.7 collective-permute-start.5
  166.2 0.7 copy-start.6
  185.6 14.2 %collective-permute-start.6 = (bf16[8,192,128]{2,1,0:T(8,128)(2,1)}, bf16[8,192,128]{2,1,0:T(8,128)(2,1)S(1)}, u32[]{:S(2)}, u32[]{:S(2)}) collective-permute-start(bf16[8,192,128]{2,1,0:T(8,128)(2,1)} %get-tuple-element.46), channel_id=1, source_target_pairs={{0,8},{8,16},{16,24},{1,9},{9,17},{17,25},{2,10},{10,18},{18,26},{... | collective-permute-start | bytes 1179656 | tf_op jit(solution)/shard_map/ppermute | solution.py:384
  187.5 12.2 %copy-start = (bf16[1,2,16,192,128]{4,3,2,1,0:T(8,128)(2,1)S(1)}, bf16[1,2,16,192,128]{4,3,2,1,0:T(8,128)(2,1)}, u32[]{:S(2)}) copy-start(bf16[1,2,16,192,128]{4,3,2,1,0:T(8,128)(2,1)} %all-gather.9.cloned.1.call-done) | copy-start | bytes 4718596
  194.9 5.8 %copy-start.9 = (bf16[8,192,128]{2,1,0:T(8,128)(2,1)S(1)}, bf16[8,192,128]{2,1,0:T(8,128)(2,1)}, u32[]{:S(2)}) copy-start(bf16[8,192,128]{2,1,0:T(8,128)(2,1)} %shard_map.82) | copy-start | bytes 1179652
  199.7 2.3 copy-start.7
  199.7 2.2 collective-permute-start.7
  202.0 0.8 copy-start.8
  202.7 11.2 %slice-start = ((bf16[3,16,192,128]{3,2,1,0:T(8,128)(2,1)}), bf16[1,16,192,128]{3,2,1,0:T(8,128)(2,1)S(1)}, s32[]{:S(2)}) async-start(bf16[3,16,192,128]{3,2,1,0:T(8,128)(2,1)} %all-gather.5.cloned.1.call-done.caches.frames), calls=%async_computation.3 | async-start | bytes 1572864 | tf_op jit(solution)/shard_map/slice | solution.py:390
Sparse Core Ops, SparseCore 0:
  10.2 32.8 all-gather.4
  45.2 24.1 all-gather.8
  71.1 24.5 all-gather.6

commit v3 on v2

--- a/solution.py
+++ b/solution.py
@@ -134,7 +134,7 @@
     outputs = out.shape[1]
     channels = x0.shape[1]
     columns = x0.shape[2]
-    pair = 4 if count % 4 == 0 else (2 if count % 2 == 0 else 1)
+    pair = 8 if count % 8 == 0 else (4 if count % 4 == 0 else (2 if count % 2 == 0 else 1))
     lanes = pair * columns
     lane = lax.broadcasted_iota(jnp.int32, (outputs, lanes), 1) % columns
 

time: 241 us -> 237 us (0.983)
  Pallas kernels: 126 us -> 119 us
    pallas_call x14, Pallas kernels: 126 us -> 119 us  [fused_conv(): pl.pallas_call(body, out_shape=shapes, in_specs=specs, out_specs=vmem if...]
  transfers between devices with their start and end apart: 11 -> 11, of which waited for: 9 -> 9; matrix products, arithmetic and copies ran while one was open for 14% -> 14% of each run, Pallas kernels for 21% -> 20%
where the time goes in v3:
time: 237 us; the launch traced here: 233 us
  Pallas kernels  119 us (50%)
  waiting for transfers between devices  42.5 us (18%)
  local copies, waits for them, and re-layouts  36.4 us (15%)
  between operations  14.4 us (6%)
  starting transfers between devices  12.4 us (5%)
  other arithmetic  8.39 us (4%)
    pallas_call x14, Pallas kernels, fused_conv(): pl.pallas_call(body, out_shape=shapes, in_specs=specs, out_specs=vmem if...  119 us
    ppermute x4, waiting for transfers between devices, shards_whole(): got = lax.ppermute(lead, 'phase', forward)  16.9 us
    all_gather x1, waiting for transfers between devices, shards_whole(): second_cache = lax.all_gather(cache_t[1], 'rows', axis=1, tiled=True)  13.6 us
    ppermute x4, starting transfers between devices, shards_whole(): got = lax.ppermute(lead, 'phase', forward)  12.3 us
    transpose x3, local copies, waits for them, and re-layouts, arrange_taps(): jnp.transpose(weight, (2, 3, 0, 1, 4)).reshape(3 * outputs, 9 * channels)  11 us
    reshape x2, local copies, waits for them, and re-layouts, arrange_taps(): jnp.transpose(weight, (2, 3, 0, 1, 4)).reshape(3 * outputs, 9 * channels)  8.77 us
    unnamed x32, local copies, waits for them, and re-layouts  7.07 us
    all_gather x1, waiting for transfers between devices, shards_whole(): lax.all_gather(jnp.stack(later), 'rows', axis=1, tiled=True)  4.78 us
  transfers between devices with their start and end apart: 11, of which 9 were waited for; matrix products, arithmetic and copies ran while one was open for 14% of the time, Pallas kernels for 20%

profile of v3, /device:TPU:4, one launch (start us, length us, event | category | flops | bytes accessed | tf_op | source)
XLA Modules:
  0.0 233.1 jit_solution(16769495692508967270)
XLA Ops:
  7.2 1.0 copy.64
  8.3 1.0 copy.65
  12.8 4.7 %slice_bitcast_fusion = (bf16[3,192,3,3,192]{4,1,0,3,2:T(8,128)(2,1)S(1)}, bf16[3,192,3,3,192]{4,1,0,3,2:T(8,128)(2,1)}) fusion(bf16[1,2,3,3,3,192,192]{6,5,4,3,2,1,0:T(8,128)(2,1)} %param.8), kind=kLoop, calls=%fused_computation | loop fusion | bytes 7962624 | tf_op jit(solution)/shard_map/transpose | solution.py:77
  17.5 2.3 copy.17
  19.8 4.5 %reshape.59.taps = bf16[576,1728]{1,0:T(8,128)(2,1)} reshape(bf16[3,192,3,3,192]{4,3,2,1,0:T(4,128)(2,1)S(1)} %copy.17) | data formatting | bytes 3981312 | tf_op jit(solution)/shard_map/reshape | solution.py:77
  24.4 0.8 copy.18.bias
  25.1 0.8 copy.19.gain
  26.7 4.0 %copy.16 = bf16[3,192,3,3,192]{4,3,2,1,0:T(4,128)(2,1)S(1)} copy(bf16[3,192,3,3,192]{4,1,0,3,2:T(8,128)(2,1)} %get-tuple-element.63) | data formatting | bytes 3981312 | tf_op jit(solution)/shard_map/transpose | solution.py:77
  30.7 4.2 %reshape.58.taps = bf16[576,1728]{1,0:T(8,128)(2,1)} reshape(bf16[3,192,3,3,192]{4,3,2,1,0:T(4,128)(2,1)S(1)} %copy.16) | data formatting | bytes 3981312 | tf_op jit(solution)/shard_map/reshape | solution.py:77
  35.0 0.8 copy.21.bias
  37.3 1.3 add_add_fusion.flags
  38.6 0.8 compare_convert_fusion.member
  39.3 3.7 %all-gather.5.cloned.1.call-done.caches.frames = bf16[3,16,192,128]{3,2,1,0:T(8,128)(2,1)} async-done(((bf16[3,2,192,128]{3,2,1,0:T(8,128)(2,1)}), bf16[3,16,192,128]{3,2,1,0:T(8,128)(2,1)}) %all-gather.5.cloned.1.call-update) | async-done | bytes 2359312 | tf_op jit(solution)/shard_map/all_gather | solution.py:337
  43.0 1.2 broadcast_in_dim.8.a_p.a_pp
  44.2 0.8 broadcast_in_dim.9.src_b.src_c
  45.0 10.9 %shard_map.77 = (bf16[16,192,128]{2,1,0:T(8,128)(2,1)}, bf16[18,192,128]{2,1,0:T(8,128)(2,1)}) custom-call(s32[5,4]{1,0:T(8,128)} %add_add_fusion.flags, bf16[3,16,192,128]{3,2,1,0:T(8,128)(2,1)} %all-gather.5.cloned.1.call-done.caches.frames, bf16[18,192,128]{2,1,0:T(8,128)(2,1)} %broadcast_in_dim.8.a_p.a_pp, ...), custom_call_target="tpu_custom_call" | custom-call | tf_op jit(solution)/shard_map/pallas_call | solution.py:282
  55.9 13.6 %all-gather.9.cloned.1.call-done = bf16[1,2,16,192,128]{4,3,2,1,0:T(8,128)(2,1)} async-done(((bf16[1,2,2,192,128]{4,3,2,1,0:T(8,128)(2,1)}), bf16[1,2,16,192,128]{4,3,2,1,0:T(8,128)(2,1)}) %all-gather.9.cloned.1.call-update) | async-done | bytes 1572880 | tf_op jit(solution)/shard_map/all_gather | solution.py:338
  69.4 7.2 %shard_map.78 = (bf16[8,192,128]{2,1,0:T(8,128)(2,1)}, bf16[18,192,128]{2,1,0:T(8,128)(2,1)}) custom-call(s32[5,4]{1,0:T(8,128)} %add_add_fusion.flags, bf16[2,16,192,128]{3,2,1,0:T(8,128)(2,1)} %bitcast.111, bf16[18,192,128]{2,1,0:T(8,128)(2,1)} %broadcast_in_dim.8.a_p.a_pp, bf16[18,192,128]{2,1,0:T(8,128)(2,1)} %broadcast_in_dim.8.a_p.a_pp, ...), custom_call_target="tpu_custom_call" | custom-call | tf_op jit(solution)/shard_map/pallas_call | solution.py:282
  76.6 3.9 %collective-permute-start = (bf16[8,192,128]{2,1,0:T(8,128)(2,1)}, bf16[8,192,128]{2,1,0:T(8,128)(2,1)S(1)}, u32[]{:S(2)}, u32[]{:S(2)}) collective-permute-start(bf16[8,192,128]{2,1,0:T(8,128)(2,1)} %get-tuple-element.32), channel_id=1, source_target_pairs={{0,8},{8,16},{16,24},{1,9},{9,17},{17,25},{2,10},{10,18},{18,26},{... | collective-permute-start | bytes 1179656 | tf_op jit(solution)/shard_map/ppermute | solution.py:384
  80.5 6.9 %shard_map.79 = bf16[8,192,128]{2,1,0:T(8,128)(2,1)} custom-call(s32[5,4]{1,0:T(8,128)} %add_add_fusion.flags, bf16[2,16,192,128]{3,2,1,0:T(8,128)(2,1)} %bitcast.112, bf16[18,192,128]{2,1,0:T(8,128)(2,1)} %broadcast_in_dim.8.a_p.a_pp, bf16[18,192,128]{2,1,0:T(8,128)(2,1)} %broadcast_in_dim.8.a_p.a_pp, ...), custom_call_target="tpu_custom_call" | custom-call | tf_op jit(solution)/shard_map/pallas_call | solution.py:282
  87.4 3.5 %collective-permute-done.src_b = bf16[8,192,128]{2,1,0:T(8,128)(2,1)S(1)} collective-permute-done((bf16[8,192,128]{2,1,0:T(8,128)(2,1)}, bf16[8,192,128]{2,1,0:T(8,128)(2,1)S(1)}, u32[]{:S(2)}, u32[]{:S(2)}) %collective-permute-start) | collective-permute-done | bytes 393248 | tf_op jit(solution)/shard_map/ppermute | solution.py:384
  90.9 4.8 %all-gather.7.cloned.1.call-done.frames = bf16[2,16,192,128]{3,2,1,0:T(8,128)(2,1)} async-done(((bf16[2,2,192,128]{3,2,1,0:T(8,128)(2,1)}), bf16[2,16,192,128]{3,2,1,0:T(8,128)(2,1)}) %all-gather.7.cloned.1.call-update) | async-done | bytes 1572880 | tf_op jit(solution)/shard_map/all_gather | solution.py:342
  96.4 10.5 %shard_map.80 = (bf16[16,192,128]{2,1,0:T(8,128)(2,1)}, bf16[18,192,128]{2,1,0:T(8,128)(2,1)}) custom-call(s32[5,4]{1,0:T(8,128)} %add_add_fusion.flags, bf16[3,16,192,128]{3,2,1,0:T(8,128)(2,1)} %all-gather.5.cloned.1.call-done.caches.frames, bf16[18,192,128]{2,1,0:T(8,128)(2,1)} %get-tuple-element.34.a_p.a_pp, ...), custom_call_target="tpu_custom_call" | custom-call | tf_op jit(solution)/shard_map/pallas_call | solution.py:282
  107.0 7.2 %shard_map.81 = (bf16[8,192,128]{2,1,0:T(8,128)(2,1)}, bf16[18,192,128]{2,1,0:T(8,128)(2,1)}) custom-call(s32[5,4]{1,0:T(8,128)} %add_add_fusion.flags, bf16[2,16,192,128]{3,2,1,0:T(8,128)(2,1)} %bitcast.113, bf16[18,192,128]{2,1,0:T(8,128)(2,1)} %get-tuple-element.31.rest_0_.a_p.a_pp, bf16[18,192,128]{2,1,0:T(8,128)(2,1)} %broadcast_in_dim.8.a_p.a_pp, ...), custom_call_target="tpu_custom_call" | custom-call | tf_op jit(solution)/shard_map/pallas_call | solution.py:282
  114.1 3.5 %collective-permute-start.2 = (bf16[8,192,128]{2,1,0:T(8,128)(2,1)}, bf16[8,192,128]{2,1,0:T(8,128)(2,1)S(1)}, u32[]{:S(2)}, u32[]{:S(2)}) collective-permute-start(bf16[8,192,128]{2,1,0:T(8,128)(2,1)} %get-tuple-element.37), channel_id=1, source_target_pairs={{0,8},{8,16},{16,24},{1,9},{9,17},{17,25},{2,10},{10,18},{18,26},{... | collective-permute-start | bytes 1179656 | tf_op jit(solution)/shard_map/ppermute | solution.py:384
  117.7 6.9 %shard_map.82 = bf16[8,192,128]{2,1,0:T(8,128)(2,1)} custom-call(s32[5,4]{1,0:T(8,128)} %add_add_fusion.flags, bf16[2,16,192,128]{3,2,1,0:T(8,128)(2,1)} %bitcast.114, bf16[18,192,128]{2,1,0:T(8,128)(2,1)} %get-tuple-element.31.rest_0_.a_p.a_pp, bf16[18,192,128]{2,1,0:T(8,128)(2,1)} %broadcast_in_dim.8.a_p.a_pp, ...), custom_call_target="tpu_custom_call" | custom-call | tf_op jit(solution)/shard_map/pallas_call | solution.py:282
  124.6 3.8 %collective-permute-done.2.src_b = bf16[8,192,128]{2,1,0:T(8,128)(2,1)S(1)} collective-permute-done((bf16[8,192,128]{2,1,0:T(8,128)(2,1)}, bf16[8,192,128]{2,1,0:T(8,128)(2,1)S(1)}, u32[]{:S(2)}, u32[]{:S(2)}) %collective-permute-start.2) | collective-permute-done | bytes 393248 | tf_op jit(solution)/shard_map/ppermute | solution.py:384
  128.4 1.7 collective-permute-done.3.src_c
  130.9 10.5 %shard_map.83 = (bf16[16,192,128]{2,1,0:T(8,128)(2,1)}, bf16[18,192,128]{2,1,0:T(8,128)(2,1)}) custom-call(s32[5,4]{1,0:T(8,128)} %add_add_fusion.flags, bf16[3,16,192,128]{3,2,1,0:T(8,128)(2,1)} %all-gather.5.cloned.1.call-done.caches.frames, bf16[18,192,128]{2,1,0:T(8,128)(2,1)} %get-tuple-element.39.a_p.a_pp, ...), custom_call_target="tpu_custom_call" | custom-call | tf_op jit(solution)/shard_map/pallas_call | solution.py:282
  141.4 7.2 %shard_map.84 = (bf16[8,192,128]{2,1,0:T(8,128)(2,1)}, bf16[18,192,128]{2,1,0:T(8,128)(2,1)}) custom-call(s32[5,4]{1,0:T(8,128)} %add_add_fusion.flags, bf16[2,16,192,128]{3,2,1,0:T(8,128)(2,1)} %bitcast.115, bf16[18,192,128]{2,1,0:T(8,128)(2,1)} %get-tuple-element.36.rest_0_.a_p.a_pp, bf16[18,192,128]{2,1,0:T(8,128)(2,1)} %get-tuple-element.31.rest_0_.a_p.a_pp, ...), custom_call_target="tpu_custom_call" | custom-call | tf_op jit(solution)/shard_map/pallas_call | solution.py:282
  148.6 2.7 %collective-permute-start.4 = (bf16[8,192,128]{2,1,0:T(8,128)(2,1)}, bf16[8,192,128]{2,1,0:T(8,128)(2,1)S(1)}, u32[]{:S(2)}, u32[]{:S(2)}) collective-permute-start(bf16[8,192,128]{2,1,0:T(8,128)(2,1)} %get-tuple-element.42), channel_id=1, source_target_pairs={{0,8},{8,16},{16,24},{1,9},{9,17},{17,25},{2,10},{10,18},{18,26},{... | collective-permute-start | bytes 1179656 | tf_op jit(solution)/shard_map/ppermute | solution.py:384
  151.3 6.8 %shard_map.85 = bf16[8,192,128]{2,1,0:T(8,128)(2,1)} custom-call(s32[5,4]{1,0:T(8,128)} %add_add_fusion.flags, bf16[2,16,192,128]{3,2,1,0:T(8,128)(2,1)} %bitcast.116, bf16[18,192,128]{2,1,0:T(8,128)(2,1)} %get-tuple-element.36.rest_0_.a_p.a_pp, bf16[18,192,128]{2,1,0:T(8,128)(2,1)} %get-tuple-element.31.rest_0_.a_p.a_pp, ...), custom_call_target="tpu_custom_call" | custom-call | tf_op jit(solution)/shard_map/pallas_call | solution.py:282
  158.2 4.6 %collective-permute-done.4.src_b = bf16[8,192,128]{2,1,0:T(8,128)(2,1)S(1)} collective-permute-done((bf16[8,192,128]{2,1,0:T(8,128)(2,1)}, bf16[8,192,128]{2,1,0:T(8,128)(2,1)S(1)}, u32[]{:S(2)}, u32[]{:S(2)}) %collective-permute-start.4) | collective-permute-done | bytes 393248 | tf_op jit(solution)/shard_map/ppermute | solution.py:384
  162.8 1.7 collective-permute-done.5.src_c
  165.2 10.5 %shard_map.86 = (bf16[16,192,128]{2,1,0:T(8,128)(2,1)}, bf16[18,192,128]{2,1,0:T(8,128)(2,1)}) custom-call(s32[5,4]{1,0:T(8,128)} %add_add_fusion.flags, bf16[3,16,192,128]{3,2,1,0:T(8,128)(2,1)} %all-gather.5.cloned.1.call-done.caches.frames, bf16[18,192,128]{2,1,0:T(8,128)(2,1)} %get-tuple-element.44.a_p.a_pp, ...), custom_call_target="tpu_custom_call" | custom-call | tf_op jit(solution)/shard_map/pallas_call | solution.py:282
  175.8 7.2 %shard_map.87 = (bf16[8,192,128]{2,1,0:T(8,128)(2,1)}, bf16[18,192,128]{2,1,0:T(8,128)(2,1)}) custom-call(s32[5,4]{1,0:T(8,128)} %add_add_fusion.flags, bf16[2,16,192,128]{3,2,1,0:T(8,128)(2,1)} %bitcast.117, bf16[18,192,128]{2,1,0:T(8,128)(2,1)} %get-tuple-element.41.rest_0_.a_p.a_pp, bf16[18,192,128]{2,1,0:T(8,128)(2,1)} %get-tuple-element.36.rest_0_.a_p.a_pp, ...), custom_call_target="tpu_custom_call" | custom-call | tf_op jit(solution)/shard_map/pallas_call | solution.py:282
  183.0 2.2 collective-permute-start.6
  185.2 6.9 %shard_map.88 = bf16[8,192,128]{2,1,0:T(8,128)(2,1)} custom-call(s32[5,4]{1,0:T(8,128)} %add_add_fusion.flags, bf16[2,16,192,128]{3,2,1,0:T(8,128)(2,1)} %bitcast.118, bf16[18,192,128]{2,1,0:T(8,128)(2,1)} %get-tuple-element.41.rest_0_.a_p.a_pp, bf16[18,192,128]{2,1,0:T(8,128)(2,1)} %get-tuple-element.36.rest_0_.a_p.a_pp, ...), custom_call_target="tpu_custom_call" | custom-call | tf_op jit(solution)/shard_map/pallas_call | solution.py:282
  192.1 5.0 %collective-permute-done.6.src_b = bf16[8,192,128]{2,1,0:T(8,128)(2,1)S(1)} collective-permute-done((bf16[8,192,128]{2,1,0:T(8,128)(2,1)}, bf16[8,192,128]{2,1,0:T(8,128)(2,1)S(1)}, u32[]{:S(2)}, u32[]{:S(2)}) %collective-permute-start.6) | collective-permute-done | bytes 393248 | tf_op jit(solution)/shard_map/ppermute | solution.py:384
  197.1 1.0 slice.52
  198.1 1.2 select_bitcast_fusion.3
  200.2 10.6 %shard_map.89 = (bf16[16,192,128]{2,1,0:T(8,128)(2,1)}, bf16[18,192,128]{2,1,0:T(8,128)(2,1)}) custom-call(s32[5,4]{1,0:T(8,128)} %add_add_fusion.flags, bf16[3,16,192,128]{3,2,1,0:T(8,128)(2,1)} %all-gather.5.cloned.1.call-done.caches.frames, bf16[18,192,128]{2,1,0:T(8,128)(2,1)} %get-tuple-element.53.a_p, ...), custom_call_target="tpu_custom_call" | custom-call | tf_op jit(solution)/shard_map/pallas_call | solution.py:282
  210.8 1.1 fusion.7
  211.9 9.8 %shard_map.90 = (bf16[16,192,128]{2,1,0:T(8,128)(2,1)}, bf16[18,192,128]{2,1,0:T(8,128)(2,1)}) custom-call(s32[5,4]{1,0:T(8,128)} %add_add_fusion.flags, bf16[2,16,192,128]{3,2,1,0:T(8,128)(2,1)} %bitcast.119, bf16[18,192,128]{2,1,0:T(8,128)(2,1)} %get-tuple-element.47.rest_0_.a_p, bf16[18,192,128]{2,1,0:T(8,128)(2,1)} %get-tuple-element.41.rest_0_.a_p.a_pp, ...), custom_call_target="tpu_custom_call" | custom-call | tf_op jit(solution)/shard_map/pallas_call | solution.py:282
  221.7 1.2 fusion.1
  223.0 1.2 copy.61
  224.1 1.2 select_bitcast_fusion.2
  225.4 0.9 copy.60
  (61 shorter events, 9.1 us)
Async XLA Ops:
  7.2 35.9 %all-gather.5.cloned.1.call-start = ((), (), s32[]{:S(2)}) async-start(), calls=%async_computation | async-start | bytes 2654208 | tf_op jit(solution)/shard_map/all_gather | solution.py:337
  10.0 59.4 %all-gather.9.cloned.1.call-start = ((), (), s32[]{:S(2)}) async-start(), calls=%async_computation.2 | async-start | bytes 1769472 | tf_op jit(solution)/shard_map/all_gather | solution.py:338
  10.8 84.9 %all-gather.7.cloned.1.call-start = ((), (), s32[]{:S(2)}) async-start(), calls=%async_computation.1 | async-start | bytes 1769472 | tf_op jit(solution)/shard_map/all_gather | solution.py:342
  19.8 4.6 %copy-start.10 = (f32[1,2,192]{2,1,0:T(2,128)S(1)}, f32[1,2,192]{2,1,0:T(2,128)}, u32[]{:S(2)}) copy-start(f32[1,2,192]{2,1,0:T(2,128)} %param.9) | copy-start | bytes 4612
  19.8 5.3 %copy-start.11 = (f32[1,2,192]{2,1,0:T(2,128)S(1)}, f32[1,2,192]{2,1,0:T(2,128)}, u32[]{:S(2)}) copy-start(f32[1,2,192]{2,1,0:T(2,128)} %param.10) | copy-start | bytes 4612
  19.8 6.1 %copy-start.12 = (f32[1,2,192]{2,1,0:T(2,128)S(1)}, f32[1,2,192]{2,1,0:T(2,128)}, u32[]{:S(2)}) copy-start(f32[1,2,192]{2,1,0:T(2,128)} %param.11) | copy-start | bytes 4612
  30.7 6.6 %copy-start.13 = (s32[4]{0:T(128)S(1)}, s32[4]{0:T(128)}, u32[]{:S(2)}) copy-start(s32[4]{0:T(128)} %pad.15.clone) | copy-start | bytes 52
  76.6 14.3 %collective-permute-start = (bf16[8,192,128]{2,1,0:T(8,128)(2,1)}, bf16[8,192,128]{2,1,0:T(8,128)(2,1)S(1)}, u32[]{:S(2)}, u32[]{:S(2)}) collective-permute-start(bf16[8,192,128]{2,1,0:T(8,128)(2,1)} %get-tuple-element.32), channel_id=1, source_target_pairs={{0,8},{8,16},{16,24},{1,9},{9,17},{17,25},{2,10},{10,18},{18,26},{... | collective-permute-start | bytes 1179656 | tf_op jit(solution)/shard_map/ppermute | solution.py:384
  90.9 4.8 %copy-start.1 = (bf16[8,192,128]{2,1,0:T(8,128)(2,1)}, bf16[8,192,128]{2,1,0:T(8,128)(2,1)S(1)}, u32[]{:S(2)}) copy-start(bf16[8,192,128]{2,1,0:T(8,128)(2,1)S(1)} %collective-permute-done.src_b) | copy-start | bytes 1179652
  90.9 4.8 %collective-permute-start.1 = (bf16[8,192,128]{2,1,0:T(8,128)(2,1)S(1)}, bf16[8,192,128]{2,1,0:T(8,128)(2,1)S(1)}, u32[]{:S(2)}, u32[]{:S(2)}) collective-permute-start(bf16[8,192,128]{2,1,0:T(8,128)(2,1)S(1)} %collective-permute-done.src_b), channel_id=1, source_target_pairs={{0,1},{1,0},{2,3},{3,2},{4,5},{5,4},{6,7},{7,6},{8,9},{9,8},{10,11... | collective-permute-start | bytes 1179656 | tf_op jit(solution)/shard_map/ppermute | solution.py:386
  95.7 0.8 copy-start.4
  114.1 14.3 %collective-permute-start.2 = (bf16[8,192,128]{2,1,0:T(8,128)(2,1)}, bf16[8,192,128]{2,1,0:T(8,128)(2,1)S(1)}, u32[]{:S(2)}, u32[]{:S(2)}) collective-permute-start(bf16[8,192,128]{2,1,0:T(8,128)(2,1)} %get-tuple-element.37), channel_id=1, source_target_pairs={{0,8},{8,16},{16,24},{1,9},{9,17},{17,25},{2,10},{10,18},{18,26},{... | collective-permute-start | bytes 1179656 | tf_op jit(solution)/shard_map/ppermute | solution.py:384
  128.4 1.7 copy-start.2
  128.4 1.7 collective-permute-start.3
  130.1 0.7 copy-start.5
  148.6 14.2 %collective-permute-start.4 = (bf16[8,192,128]{2,1,0:T(8,128)(2,1)}, bf16[8,192,128]{2,1,0:T(8,128)(2,1)S(1)}, u32[]{:S(2)}, u32[]{:S(2)}) collective-permute-start(bf16[8,192,128]{2,1,0:T(8,128)(2,1)} %get-tuple-element.42), channel_id=1, source_target_pairs={{0,8},{8,16},{16,24},{1,9},{9,17},{17,25},{2,10},{10,18},{18,26},{... | collective-permute-start | bytes 1179656 | tf_op jit(solution)/shard_map/ppermute | solution.py:384
  162.8 1.7 copy-start.3
  162.8 1.7 collective-permute-start.5
  164.5 0.7 copy-start.6
  183.0 14.2 %collective-permute-start.6 = (bf16[8,192,128]{2,1,0:T(8,128)(2,1)}, bf16[8,192,128]{2,1,0:T(8,128)(2,1)S(1)}, u32[]{:S(2)}, u32[]{:S(2)}) collective-permute-start(bf16[8,192,128]{2,1,0:T(8,128)(2,1)} %get-tuple-element.46), channel_id=1, source_target_pairs={{0,8},{8,16},{16,24},{1,9},{9,17},{17,25},{2,10},{10,18},{18,26},{... | collective-permute-start | bytes 1179656 | tf_op jit(solution)/shard_map/ppermute | solution.py:384
  185.2 12.0 %copy-start = (bf16[1,2,16,192,128]{4,3,2,1,0:T(8,128)(2,1)S(1)}, bf16[1,2,16,192,128]{4,3,2,1,0:T(8,128)(2,1)}, u32[]{:S(2)}) copy-start(bf16[1,2,16,192,128]{4,3,2,1,0:T(8,128)(2,1)} %all-gather.9.cloned.1.call-done) | copy-start | bytes 4718596
  192.1 6.0 %copy-start.9 = (bf16[8,192,128]{2,1,0:T(8,128)(2,1)S(1)}, bf16[8,192,128]{2,1,0:T(8,128)(2,1)}, u32[]{:S(2)}) copy-start(bf16[8,192,128]{2,1,0:T(8,128)(2,1)} %shard_map.82) | copy-start | bytes 1179652
  197.1 2.3 copy-start.7
  197.1 2.2 collective-permute-start.7
  199.4 0.8 copy-start.8
  200.1 10.6 %slice-start = ((bf16[3,16,192,128]{3,2,1,0:T(8,128)(2,1)}), bf16[1,16,192,128]{3,2,1,0:T(8,128)(2,1)S(1)}, s32[]{:S(2)}) async-start(bf16[3,16,192,128]{3,2,1,0:T(8,128)(2,1)} %all-gather.5.cloned.1.call-done.caches.frames), calls=%async_computation.3 | async-start | bytes 1572864 | tf_op jit(solution)/shard_map/slice | solution.py:390
Sparse Core Ops, SparseCore 0:
  10.2 32.8 all-gather.4
  45.2 24.1 all-gather.8
  71.0 24.5 all-gather.6

commit v4 on v3

--- a/solution.py
+++ b/solution.py
@@ -199,6 +199,17 @@
     @pl.when(mode == 2)
     def _():
         begin([(src_c, top), (src_b, bottom)], 0)
+
+    if kind in ("lead", "tail"):
+        base = core * half if kind == "lead" else (1 - core) * half
+        low = base - 1 + (base == 0).astype(jnp.int32)
+        length = half + 1
+
+        def inner(x, rim=1):
+            return x.at[pl.ds(low + rim, length)]
+
+        inner0, inner1 = inner(x0), inner(x1)
+        c0, c1 = inner(c0, 0), inner(c1, 0)
 
     @pl.when(first == 1)
     def _():

time: 237 us -> 237 us (level)
  transfers between devices with their start and end apart: 11 -> 11, of which waited for: 9 -> 9; matrix products, arithmetic and copies ran while one was open for 14% -> 14% of each run, Pallas kernels for 20% -> 19%
where the time goes in v4:
time: 237 us; the launch traced here: 233 us
  Pallas kernels  118 us (50%)
  waiting for transfers between devices  43.4 us (18%)
  local copies, waits for them, and re-layouts  36.4 us (15%)
  between operations  14.4 us (6%)
  starting transfers between devices  12.4 us (5%)
  other arithmetic  8.39 us (4%)
    pallas_call x14, Pallas kernels, fused_conv(): pl.pallas_call(body, out_shape=shapes, in_specs=specs, out_specs=vmem if...  118 us
    ppermute x4, waiting for transfers between devices, shards_whole(): got = lax.ppermute(lead, 'phase', forward)  17.8 us
    all_gather x1, waiting for transfers between devices, shards_whole(): second_cache = lax.all_gather(cache_t[1], 'rows', axis=1, tiled=True)  13.6 us
    ppermute x4, starting transfers between devices, shards_whole(): got = lax.ppermute(lead, 'phase', forward)  12.3 us
    transpose x3, local copies, waits for them, and re-layouts, arrange_taps(): jnp.transpose(weight, (2, 3, 0, 1, 4)).reshape(3 * outputs, 9 * channels)  11 us
    reshape x2, local copies, waits for them, and re-layouts, arrange_taps(): jnp.transpose(weight, (2, 3, 0, 1, 4)).reshape(3 * outputs, 9 * channels)  8.77 us
    unnamed x32, local copies, waits for them, and re-layouts  7.07 us
    all_gather x1, waiting for transfers between devices, shards_whole(): lax.all_gather(jnp.stack(later), 'rows', axis=1, tiled=True)  4.78 us
  transfers between devices with their start and end apart: 11, of which 9 were waited for; matrix products, arithmetic and copies ran while one was open for 14% of the time, Pallas kernels for 19%

profile of v4, /device:TPU:4, one launch (start us, length us, event | category | flops | bytes accessed | tf_op | source)
XLA Modules:
  0.0 233.1 jit_solution(2790683682795999800)
XLA Ops:
  7.2 1.0 copy.64
  8.3 1.0 copy.65
  12.8 4.7 %slice_bitcast_fusion = (bf16[3,192,3,3,192]{4,1,0,3,2:T(8,128)(2,1)S(1)}, bf16[3,192,3,3,192]{4,1,0,3,2:T(8,128)(2,1)}) fusion(bf16[1,2,3,3,3,192,192]{6,5,4,3,2,1,0:T(8,128)(2,1)} %param.8), kind=kLoop, calls=%fused_computation | loop fusion | bytes 7962624 | tf_op jit(solution)/shard_map/transpose | solution.py:77
  17.5 2.3 copy.17
  19.8 4.5 %reshape.59.taps = bf16[576,1728]{1,0:T(8,128)(2,1)} reshape(bf16[3,192,3,3,192]{4,3,2,1,0:T(4,128)(2,1)S(1)} %copy.17) | data formatting | bytes 3981312 | tf_op jit(solution)/shard_map/reshape | solution.py:77
  24.4 0.8 copy.18.bias
  25.1 0.8 copy.19.gain
  26.7 4.0 %copy.16 = bf16[3,192,3,3,192]{4,3,2,1,0:T(4,128)(2,1)S(1)} copy(bf16[3,192,3,3,192]{4,1,0,3,2:T(8,128)(2,1)} %get-tuple-element.63) | data formatting | bytes 3981312 | tf_op jit(solution)/shard_map/transpose | solution.py:77
  30.7 4.2 %reshape.58.taps = bf16[576,1728]{1,0:T(8,128)(2,1)} reshape(bf16[3,192,3,3,192]{4,3,2,1,0:T(4,128)(2,1)S(1)} %copy.16) | data formatting | bytes 3981312 | tf_op jit(solution)/shard_map/reshape | solution.py:77
  35.0 0.8 copy.21.bias
  37.3 1.3 add_add_fusion.flags
  38.6 0.8 compare_convert_fusion.member
  39.3 3.7 %all-gather.5.cloned.1.call-done.caches.frames = bf16[3,16,192,128]{3,2,1,0:T(8,128)(2,1)} async-done(((bf16[3,2,192,128]{3,2,1,0:T(8,128)(2,1)}), bf16[3,16,192,128]{3,2,1,0:T(8,128)(2,1)}) %all-gather.5.cloned.1.call-update) | async-done | bytes 2359312 | tf_op jit(solution)/shard_map/all_gather | solution.py:348
  43.0 1.2 broadcast_in_dim.8.a_p.a_pp
  44.2 0.8 broadcast_in_dim.9.src_b.src_c
  45.0 10.9 %shard_map.77 = (bf16[16,192,128]{2,1,0:T(8,128)(2,1)}, bf16[18,192,128]{2,1,0:T(8,128)(2,1)}) custom-call(s32[5,4]{1,0:T(8,128)} %add_add_fusion.flags, bf16[3,16,192,128]{3,2,1,0:T(8,128)(2,1)} %all-gather.5.cloned.1.call-done.caches.frames, bf16[18,192,128]{2,1,0:T(8,128)(2,1)} %broadcast_in_dim.8.a_p.a_pp, ...), custom_call_target="tpu_custom_call" | custom-call | tf_op jit(solution)/shard_map/pallas_call | solution.py:293
  55.9 13.6 %all-gather.9.cloned.1.call-done = bf16[1,2,16,192,128]{4,3,2,1,0:T(8,128)(2,1)} async-done(((bf16[1,2,2,192,128]{4,3,2,1,0:T(8,128)(2,1)}), bf16[1,2,16,192,128]{4,3,2,1,0:T(8,128)(2,1)}) %all-gather.9.cloned.1.call-update) | async-done | bytes 1572880 | tf_op jit(solution)/shard_map/all_gather | solution.py:349
  69.4 7.2 %shard_map.78 = (bf16[8,192,128]{2,1,0:T(8,128)(2,1)}, bf16[18,192,128]{2,1,0:T(8,128)(2,1)}) custom-call(s32[5,4]{1,0:T(8,128)} %add_add_fusion.flags, bf16[2,16,192,128]{3,2,1,0:T(8,128)(2,1)} %bitcast.111, bf16[18,192,128]{2,1,0:T(8,128)(2,1)} %broadcast_in_dim.8.a_p.a_pp, bf16[18,192,128]{2,1,0:T(8,128)(2,1)} %broadcast_in_dim.8.a_p.a_pp, ...), custom_call_target="tpu_custom_call" | custom-call | tf_op jit(solution)/shard_map/pallas_call | solution.py:293
  76.6 3.9 %collective-permute-start = (bf16[8,192,128]{2,1,0:T(8,128)(2,1)}, bf16[8,192,128]{2,1,0:T(8,128)(2,1)S(1)}, u32[]{:S(2)}, u32[]{:S(2)}) collective-permute-start(bf16[8,192,128]{2,1,0:T(8,128)(2,1)} %get-tuple-element.32), channel_id=1, source_target_pairs={{0,8},{8,16},{16,24},{1,9},{9,17},{17,25},{2,10},{10,18},{18,26},{... | collective-permute-start | bytes 1179656 | tf_op jit(solution)/shard_map/ppermute | solution.py:395
  80.5 6.6 %shard_map.79 = bf16[8,192,128]{2,1,0:T(8,128)(2,1)} custom-call(s32[5,4]{1,0:T(8,128)} %add_add_fusion.flags, bf16[2,16,192,128]{3,2,1,0:T(8,128)(2,1)} %bitcast.112, bf16[18,192,128]{2,1,0:T(8,128)(2,1)} %broadcast_in_dim.8.a_p.a_pp, bf16[18,192,128]{2,1,0:T(8,128)(2,1)} %broadcast_in_dim.8.a_p.a_pp, ...), custom_call_target="tpu_custom_call" | custom-call | tf_op jit(solution)/shard_map/pallas_call | solution.py:293
  87.2 3.7 %collective-permute-done.src_b = bf16[8,192,128]{2,1,0:T(8,128)(2,1)S(1)} collective-permute-done((bf16[8,192,128]{2,1,0:T(8,128)(2,1)}, bf16[8,192,128]{2,1,0:T(8,128)(2,1)S(1)}, u32[]{:S(2)}, u32[]{:S(2)}) %collective-permute-start) | collective-permute-done | bytes 393248 | tf_op jit(solution)/shard_map/ppermute | solution.py:395
  90.9 4.8 %all-gather.7.cloned.1.call-done.frames = bf16[2,16,192,128]{3,2,1,0:T(8,128)(2,1)} async-done(((bf16[2,2,192,128]{3,2,1,0:T(8,128)(2,1)}), bf16[2,16,192,128]{3,2,1,0:T(8,128)(2,1)}) %all-gather.7.cloned.1.call-update) | async-done | bytes 1572880 | tf_op jit(solution)/shard_map/all_gather | solution.py:353
  96.4 10.5 %shard_map.80 = (bf16[16,192,128]{2,1,0:T(8,128)(2,1)}, bf16[18,192,128]{2,1,0:T(8,128)(2,1)}) custom-call(s32[5,4]{1,0:T(8,128)} %add_add_fusion.flags, bf16[3,16,192,128]{3,2,1,0:T(8,128)(2,1)} %all-gather.5.cloned.1.call-done.caches.frames, bf16[18,192,128]{2,1,0:T(8,128)(2,1)} %get-tuple-element.34.a_p.a_pp, ...), custom_call_target="tpu_custom_call" | custom-call | tf_op jit(solution)/shard_map/pallas_call | solution.py:293
  107.0 7.2 %shard_map.81 = (bf16[8,192,128]{2,1,0:T(8,128)(2,1)}, bf16[18,192,128]{2,1,0:T(8,128)(2,1)}) custom-call(s32[5,4]{1,0:T(8,128)} %add_add_fusion.flags, bf16[2,16,192,128]{3,2,1,0:T(8,128)(2,1)} %bitcast.113, bf16[18,192,128]{2,1,0:T(8,128)(2,1)} %get-tuple-element.31.rest_0_.a_p.a_pp, bf16[18,192,128]{2,1,0:T(8,128)(2,1)} %broadcast_in_dim.8.a_p.a_pp, ...), custom_call_target="tpu_custom_call" | custom-call | tf_op jit(solution)/shard_map/pallas_call | solution.py:293
  114.2 3.5 %collective-permute-start.2 = (bf16[8,192,128]{2,1,0:T(8,128)(2,1)}, bf16[8,192,128]{2,1,0:T(8,128)(2,1)S(1)}, u32[]{:S(2)}, u32[]{:S(2)}) collective-permute-start(bf16[8,192,128]{2,1,0:T(8,128)(2,1)} %get-tuple-element.37), channel_id=1, source_target_pairs={{0,8},{8,16},{16,24},{1,9},{9,17},{17,25},{2,10},{10,18},{18,26},{... | collective-permute-start | bytes 1179656 | tf_op jit(solution)/shard_map/ppermute | solution.py:395
  117.7 6.6 %shard_map.82 = bf16[8,192,128]{2,1,0:T(8,128)(2,1)} custom-call(s32[5,4]{1,0:T(8,128)} %add_add_fusion.flags, bf16[2,16,192,128]{3,2,1,0:T(8,128)(2,1)} %bitcast.114, bf16[18,192,128]{2,1,0:T(8,128)(2,1)} %get-tuple-element.31.rest_0_.a_p.a_pp, bf16[18,192,128]{2,1,0:T(8,128)(2,1)} %broadcast_in_dim.8.a_p.a_pp, ...), custom_call_target="tpu_custom_call" | custom-call | tf_op jit(solution)/shard_map/pallas_call | solution.py:293
  124.3 4.1 %collective-permute-done.2.src_b = bf16[8,192,128]{2,1,0:T(8,128)(2,1)S(1)} collective-permute-done((bf16[8,192,128]{2,1,0:T(8,128)(2,1)}, bf16[8,192,128]{2,1,0:T(8,128)(2,1)S(1)}, u32[]{:S(2)}, u32[]{:S(2)}) %collective-permute-start.2) | collective-permute-done | bytes 393248 | tf_op jit(solution)/shard_map/ppermute | solution.py:395
  128.4 1.7 collective-permute-done.3.src_c
  130.9 10.5 %shard_map.83 = (bf16[16,192,128]{2,1,0:T(8,128)(2,1)}, bf16[18,192,128]{2,1,0:T(8,128)(2,1)}) custom-call(s32[5,4]{1,0:T(8,128)} %add_add_fusion.flags, bf16[3,16,192,128]{3,2,1,0:T(8,128)(2,1)} %all-gather.5.cloned.1.call-done.caches.frames, bf16[18,192,128]{2,1,0:T(8,128)(2,1)} %get-tuple-element.39.a_p.a_pp, ...), custom_call_target="tpu_custom_call" | custom-call | tf_op jit(solution)/shard_map/pallas_call | solution.py:293
  141.4 7.2 %shard_map.84 = (bf16[8,192,128]{2,1,0:T(8,128)(2,1)}, bf16[18,192,128]{2,1,0:T(8,128)(2,1)}) custom-call(s32[5,4]{1,0:T(8,128)} %add_add_fusion.flags, bf16[2,16,192,128]{3,2,1,0:T(8,128)(2,1)} %bitcast.115, bf16[18,192,128]{2,1,0:T(8,128)(2,1)} %get-tuple-element.36.rest_0_.a_p.a_pp, bf16[18,192,128]{2,1,0:T(8,128)(2,1)} %get-tuple-element.31.rest_0_.a_p.a_pp, ...), custom_call_target="tpu_custom_call" | custom-call | tf_op jit(solution)/shard_map/pallas_call | solution.py:293
  148.6 2.7 %collective-permute-start.4 = (bf16[8,192,128]{2,1,0:T(8,128)(2,1)}, bf16[8,192,128]{2,1,0:T(8,128)(2,1)S(1)}, u32[]{:S(2)}, u32[]{:S(2)}) collective-permute-start(bf16[8,192,128]{2,1,0:T(8,128)(2,1)} %get-tuple-element.42), channel_id=1, source_target_pairs={{0,8},{8,16},{16,24},{1,9},{9,17},{17,25},{2,10},{10,18},{18,26},{... | collective-permute-start | bytes 1179656 | tf_op jit(solution)/shard_map/ppermute | solution.py:395
  151.3 6.6 %shard_map.85 = bf16[8,192,128]{2,1,0:T(8,128)(2,1)} custom-call(s32[5,4]{1,0:T(8,128)} %add_add_fusion.flags, bf16[2,16,192,128]{3,2,1,0:T(8,128)(2,1)} %bitcast.116, bf16[18,192,128]{2,1,0:T(8,128)(2,1)} %get-tuple-element.36.rest_0_.a_p.a_pp, bf16[18,192,128]{2,1,0:T(8,128)(2,1)} %get-tuple-element.31.rest_0_.a_p.a_pp, ...), custom_call_target="tpu_custom_call" | custom-call | tf_op jit(solution)/shard_map/pallas_call | solution.py:293
  157.9 4.8 %collective-permute-done.4.src_b = bf16[8,192,128]{2,1,0:T(8,128)(2,1)S(1)} collective-permute-done((bf16[8,192,128]{2,1,0:T(8,128)(2,1)}, bf16[8,192,128]{2,1,0:T(8,128)(2,1)S(1)}, u32[]{:S(2)}, u32[]{:S(2)}) %collective-permute-start.4) | collective-permute-done | bytes 393248 | tf_op jit(solution)/shard_map/ppermute | solution.py:395
  162.8 1.7 collective-permute-done.5.src_c
  165.2 10.6 %shard_map.86 = (bf16[16,192,128]{2,1,0:T(8,128)(2,1)}, bf16[18,192,128]{2,1,0:T(8,128)(2,1)}) custom-call(s32[5,4]{1,0:T(8,128)} %add_add_fusion.flags, bf16[3,16,192,128]{3,2,1,0:T(8,128)(2,1)} %all-gather.5.cloned.1.call-done.caches.frames, bf16[18,192,128]{2,1,0:T(8,128)(2,1)} %get-tuple-element.44.a_p.a_pp, ...), custom_call_target="tpu_custom_call" | custom-call | tf_op jit(solution)/shard_map/pallas_call | solution.py:293
  175.8 7.2 %shard_map.87 = (bf16[8,192,128]{2,1,0:T(8,128)(2,1)}, bf16[18,192,128]{2,1,0:T(8,128)(2,1)}) custom-call(s32[5,4]{1,0:T(8,128)} %add_add_fusion.flags, bf16[2,16,192,128]{3,2,1,0:T(8,128)(2,1)} %bitcast.117, bf16[18,192,128]{2,1,0:T(8,128)(2,1)} %get-tuple-element.41.rest_0_.a_p.a_pp, bf16[18,192,128]{2,1,0:T(8,128)(2,1)} %get-tuple-element.36.rest_0_.a_p.a_pp, ...), custom_call_target="tpu_custom_call" | custom-call | tf_op jit(solution)/shard_map/pallas_call | solution.py:293
  183.0 2.2 collective-permute-start.6
  185.2 6.7 %shard_map.88 = bf16[8,192,128]{2,1,0:T(8,128)(2,1)} custom-call(s32[5,4]{1,0:T(8,128)} %add_add_fusion.flags, bf16[2,16,192,128]{3,2,1,0:T(8,128)(2,1)} %bitcast.118, bf16[18,192,128]{2,1,0:T(8,128)(2,1)} %get-tuple-element.41.rest_0_.a_p.a_pp, bf16[18,192,128]{2,1,0:T(8,128)(2,1)} %get-tuple-element.36.rest_0_.a_p.a_pp, ...), custom_call_target="tpu_custom_call" | custom-call | tf_op jit(solution)/shard_map/pallas_call | solution.py:293
  191.9 5.2 %collective-permute-done.6.src_b = bf16[8,192,128]{2,1,0:T(8,128)(2,1)S(1)} collective-permute-done((bf16[8,192,128]{2,1,0:T(8,128)(2,1)}, bf16[8,192,128]{2,1,0:T(8,128)(2,1)S(1)}, u32[]{:S(2)}, u32[]{:S(2)}) %collective-permute-start.6) | collective-permute-done | bytes 393248 | tf_op jit(solution)/shard_map/ppermute | solution.py:395
  197.1 1.0 slice.52
  198.1 1.2 select_bitcast_fusion.3
  200.2 10.6 %shard_map.89 = (bf16[16,192,128]{2,1,0:T(8,128)(2,1)}, bf16[18,192,128]{2,1,0:T(8,128)(2,1)}) custom-call(s32[5,4]{1,0:T(8,128)} %add_add_fusion.flags, bf16[3,16,192,128]{3,2,1,0:T(8,128)(2,1)} %all-gather.5.cloned.1.call-done.caches.frames, bf16[18,192,128]{2,1,0:T(8,128)(2,1)} %get-tuple-element.53.a_p, ...), custom_call_target="tpu_custom_call" | custom-call | tf_op jit(solution)/shard_map/pallas_call | solution.py:293
  210.8 1.1 fusion.7
  211.9 9.8 %shard_map.90 = (bf16[16,192,128]{2,1,0:T(8,128)(2,1)}, bf16[18,192,128]{2,1,0:T(8,128)(2,1)}) custom-call(s32[5,4]{1,0:T(8,128)} %add_add_fusion.flags, bf16[2,16,192,128]{3,2,1,0:T(8,128)(2,1)} %bitcast.119, bf16[18,192,128]{2,1,0:T(8,128)(2,1)} %get-tuple-element.47.rest_0_.a_p, bf16[18,192,128]{2,1,0:T(8,128)(2,1)} %get-tuple-element.41.rest_0_.a_p.a_pp, ...), custom_call_target="tpu_custom_call" | custom-call | tf_op jit(solution)/shard_map/pallas_call | solution.py:293
  221.7 1.2 fusion.1
  223.0 1.2 copy.61
  224.1 1.2 select_bitcast_fusion.2
  225.4 0.9 copy.60
  (61 shorter events, 9.1 us)
Async XLA Ops:
  7.2 35.9 %all-gather.5.cloned.1.call-start = ((), (), s32[]{:S(2)}) async-start(), calls=%async_computation | async-start | bytes 2654208 | tf_op jit(solution)/shard_map/all_gather | solution.py:348
  10.0 59.4 %all-gather.9.cloned.1.call-start = ((), (), s32[]{:S(2)}) async-start(), calls=%async_computation.2 | async-start | bytes 1769472 | tf_op jit(solution)/shard_map/all_gather | solution.py:349
  10.8 84.9 %all-gather.7.cloned.1.call-start = ((), (), s32[]{:S(2)}) async-start(), calls=%async_computation.1 | async-start | bytes 1769472 | tf_op jit(solution)/shard_map/all_gather | solution.py:353
  19.8 4.6 %copy-start.10 = (f32[1,2,192]{2,1,0:T(2,128)S(1)}, f32[1,2,192]{2,1,0:T(2,128)}, u32[]{:S(2)}) copy-start(f32[1,2,192]{2,1,0:T(2,128)} %param.9) | copy-start | bytes 4612
  19.8 5.3 %copy-start.11 = (f32[1,2,192]{2,1,0:T(2,128)S(1)}, f32[1,2,192]{2,1,0:T(2,128)}, u32[]{:S(2)}) copy-start(f32[1,2,192]{2,1,0:T(2,128)} %param.10) | copy-start | bytes 4612
  19.8 6.1 %copy-start.12 = (f32[1,2,192]{2,1,0:T(2,128)S(1)}, f32[1,2,192]{2,1,0:T(2,128)}, u32[]{:S(2)}) copy-start(f32[1,2,192]{2,1,0:T(2,128)} %param.11) | copy-start | bytes 4612
  30.7 6.6 %copy-start.13 = (s32[4]{0:T(128)S(1)}, s32[4]{0:T(128)}, u32[]{:S(2)}) copy-start(s32[4]{0:T(128)} %pad.15.clone) | copy-start | bytes 52
  76.6 14.3 %collective-permute-start = (bf16[8,192,128]{2,1,0:T(8,128)(2,1)}, bf16[8,192,128]{2,1,0:T(8,128)(2,1)S(1)}, u32[]{:S(2)}, u32[]{:S(2)}) collective-permute-start(bf16[8,192,128]{2,1,0:T(8,128)(2,1)} %get-tuple-element.32), channel_id=1, source_target_pairs={{0,8},{8,16},{16,24},{1,9},{9,17},{17,25},{2,10},{10,18},{18,26},{... | collective-permute-start | bytes 1179656 | tf_op jit(solution)/shard_map/ppermute | solution.py:395
  90.9 4.8 %copy-start.1 = (bf16[8,192,128]{2,1,0:T(8,128)(2,1)}, bf16[8,192,128]{2,1,0:T(8,128)(2,1)S(1)}, u32[]{:S(2)}) copy-start(bf16[8,192,128]{2,1,0:T(8,128)(2,1)S(1)} %collective-permute-done.src_b) | copy-start | bytes 1179652
  90.9 4.8 %collective-permute-start.1 = (bf16[8,192,128]{2,1,0:T(8,128)(2,1)S(1)}, bf16[8,192,128]{2,1,0:T(8,128)(2,1)S(1)}, u32[]{:S(2)}, u32[]{:S(2)}) collective-permute-start(bf16[8,192,128]{2,1,0:T(8,128)(2,1)S(1)} %collective-permute-done.src_b), channel_id=1, source_target_pairs={{0,1},{1,0},{2,3},{3,2},{4,5},{5,4},{6,7},{7,6},{8,9},{9,8},{10,11... | collective-permute-start | bytes 1179656 | tf_op jit(solution)/shard_map/ppermute | solution.py:397
  95.7 0.8 copy-start.4
  114.2 14.3 %collective-permute-start.2 = (bf16[8,192,128]{2,1,0:T(8,128)(2,1)}, bf16[8,192,128]{2,1,0:T(8,128)(2,1)S(1)}, u32[]{:S(2)}, u32[]{:S(2)}) collective-permute-start(bf16[8,192,128]{2,1,0:T(8,128)(2,1)} %get-tuple-element.37), channel_id=1, source_target_pairs={{0,8},{8,16},{16,24},{1,9},{9,17},{17,25},{2,10},{10,18},{18,26},{... | collective-permute-start | bytes 1179656 | tf_op jit(solution)/shard_map/ppermute | solution.py:395
  128.4 1.7 copy-start.2
  128.4 1.7 collective-permute-start.3
  130.1 0.7 copy-start.5
  148.6 14.2 %collective-permute-start.4 = (bf16[8,192,128]{2,1,0:T(8,128)(2,1)}, bf16[8,192,128]{2,1,0:T(8,128)(2,1)S(1)}, u32[]{:S(2)}, u32[]{:S(2)}) collective-permute-start(bf16[8,192,128]{2,1,0:T(8,128)(2,1)} %get-tuple-element.42), channel_id=1, source_target_pairs={{0,8},{8,16},{16,24},{1,9},{9,17},{17,25},{2,10},{10,18},{18,26},{... | collective-permute-start | bytes 1179656 | tf_op jit(solution)/shard_map/ppermute | solution.py:395
  162.8 1.7 copy-start.3
  162.8 1.7 collective-permute-start.5
  164.5 0.7 copy-start.6
  183.0 14.2 %collective-permute-start.6 = (bf16[8,192,128]{2,1,0:T(8,128)(2,1)}, bf16[8,192,128]{2,1,0:T(8,128)(2,1)S(1)}, u32[]{:S(2)}, u32[]{:S(2)}) collective-permute-start(bf16[8,192,128]{2,1,0:T(8,128)(2,1)} %get-tuple-element.46), channel_id=1, source_target_pairs={{0,8},{8,16},{16,24},{1,9},{9,17},{17,25},{2,10},{10,18},{18,26},{... | collective-permute-start | bytes 1179656 | tf_op jit(solution)/shard_map/ppermute | solution.py:395
  185.2 12.0 %copy-start = (bf16[1,2,16,192,128]{4,3,2,1,0:T(8,128)(2,1)S(1)}, bf16[1,2,16,192,128]{4,3,2,1,0:T(8,128)(2,1)}, u32[]{:S(2)}) copy-start(bf16[1,2,16,192,128]{4,3,2,1,0:T(8,128)(2,1)} %all-gather.9.cloned.1.call-done) | copy-start | bytes 4718596
  191.9 6.3 %copy-start.9 = (bf16[8,192,128]{2,1,0:T(8,128)(2,1)S(1)}, bf16[8,192,128]{2,1,0:T(8,128)(2,1)}, u32[]{:S(2)}) copy-start(bf16[8,192,128]{2,1,0:T(8,128)(2,1)} %shard_map.82) | copy-start | bytes 1179652
  197.1 2.3 copy-start.7
  197.1 2.2 collective-permute-start.7
  199.4 0.8 copy-start.8
  200.1 10.6 %slice-start = ((bf16[3,16,192,128]{3,2,1,0:T(8,128)(2,1)}), bf16[1,16,192,128]{3,2,1,0:T(8,128)(2,1)S(1)}, s32[]{:S(2)}) async-start(bf16[3,16,192,128]{3,2,1,0:T(8,128)(2,1)} %all-gather.5.cloned.1.call-done.caches.frames), calls=%async_computation.3 | async-start | bytes 1572864 | tf_op jit(solution)/shard_map/slice | solution.py:401
Sparse Core Ops, SparseCore 0:
  10.2 32.8 all-gather.4
  45.2 24.1 all-gather.8
  71.0 24.5 all-gather.6

commit v5 on v3

--- a/solution.py
+++ b/solution.py
@@ -134,7 +134,7 @@
     outputs = out.shape[1]
     channels = x0.shape[1]
     columns = x0.shape[2]
-    pair = 8 if count % 8 == 0 else (4 if count % 4 == 0 else (2 if count % 2 == 0 else 1))
+    pair = next(p for p in (16, 8, 4, 2, 1) if count % p == 0)
     lanes = pair * columns
     lane = lax.broadcasted_iota(jnp.int32, (outputs, lanes), 1) % columns
 

time: 237 us -> 236 us (level)
  no operation moved by 1% of the time
where the time goes in v5:
time: 236 us; the launch traced here: 232 us
  Pallas kernels  117 us (50%)
  waiting for transfers between devices  43 us (18%)
  local copies, waits for them, and re-layouts  36.3 us (15%)
  between operations  14.3 us (6%)
  starting transfers between devices  12.3 us (5%)
  other arithmetic  8.39 us (4%)
    pallas_call x14, Pallas kernels, fused_conv(): pl.pallas_call(body, out_shape=shapes, in_specs=specs, out_specs=vmem if...  117 us
    ppermute x4, waiting for transfers between devices, shards_whole(): got = lax.ppermute(lead, 'phase', forward)  17.1 us
    all_gather x1, waiting for transfers between devices, shards_whole(): second_cache = lax.all_gather(cache_t[1], 'rows', axis=1, tiled=True)  13.9 us
    ppermute x4, starting transfers between devices, shards_whole(): got = lax.ppermute(lead, 'phase', forward)  12.1 us
    transpose x3, local copies, waits for them, and re-layouts, arrange_taps(): jnp.transpose(weight, (2, 3, 0, 1, 4)).reshape(3 * outputs, 9 * channels)  11 us
    reshape x2, local copies, waits for them, and re-layouts, arrange_taps(): jnp.transpose(weight, (2, 3, 0, 1, 4)).reshape(3 * outputs, 9 * channels)  8.65 us
    unnamed x32, local copies, waits for them, and re-layouts  7.07 us
    all_gather x1, waiting for transfers between devices, shards_whole(): lax.all_gather(jnp.stack(later), 'rows', axis=1, tiled=True)  4.78 us
  transfers between devices with their start and end apart: 11, of which 9 were waited for; matrix products, arithmetic and copies ran while one was open for 14% of the time, Pallas kernels for 20%

profile of v5, /device:TPU:4, one launch (start us, length us, event | category | flops | bytes accessed | tf_op | source)
XLA Modules:
  0.0 231.6 jit_solution(6436811642761800747)
XLA Ops:
  7.2 1.0 copy.64
  8.3 1.0 copy.65
  12.8 4.7 %slice_bitcast_fusion = (bf16[3,192,3,3,192]{4,1,0,3,2:T(8,128)(2,1)S(1)}, bf16[3,192,3,3,192]{4,1,0,3,2:T(8,128)(2,1)}) fusion(bf16[1,2,3,3,3,192,192]{6,5,4,3,2,1,0:T(8,128)(2,1)} %param.8), kind=kLoop, calls=%fused_computation | loop fusion | bytes 7962624 | tf_op jit(solution)/shard_map/transpose | solution.py:77
  17.5 2.3 copy.17
  19.8 4.4 %reshape.59.taps = bf16[576,1728]{1,0:T(8,128)(2,1)} reshape(bf16[3,192,3,3,192]{4,3,2,1,0:T(4,128)(2,1)S(1)} %copy.17) | data formatting | bytes 3981312 | tf_op jit(solution)/shard_map/reshape | solution.py:77
  24.2 0.8 copy.18.bias
  25.0 0.8 copy.19.gain
  26.5 4.1 %copy.16 = bf16[3,192,3,3,192]{4,3,2,1,0:T(4,128)(2,1)S(1)} copy(bf16[3,192,3,3,192]{4,1,0,3,2:T(8,128)(2,1)} %get-tuple-element.63) | data formatting | bytes 3981312 | tf_op jit(solution)/shard_map/transpose | solution.py:77
  30.6 4.2 %reshape.58.taps = bf16[576,1728]{1,0:T(8,128)(2,1)} reshape(bf16[3,192,3,3,192]{4,3,2,1,0:T(4,128)(2,1)S(1)} %copy.16) | data formatting | bytes 3981312 | tf_op jit(solution)/shard_map/reshape | solution.py:77
  34.9 0.8 copy.21.bias
  37.2 1.3 add_add_fusion.flags
  38.5 0.8 compare_convert_fusion.member
  39.3 3.8 %all-gather.5.cloned.1.call-done.caches.frames = bf16[3,16,192,128]{3,2,1,0:T(8,128)(2,1)} async-done(((bf16[3,2,192,128]{3,2,1,0:T(8,128)(2,1)}), bf16[3,16,192,128]{3,2,1,0:T(8,128)(2,1)}) %all-gather.5.cloned.1.call-update) | async-done | bytes 2359312 | tf_op jit(solution)/shard_map/all_gather | solution.py:337
  43.0 1.2 broadcast_in_dim.8.a_p.a_pp
  44.2 0.8 broadcast_in_dim.9.src_b.src_c
  45.0 10.6 %shard_map.77 = (bf16[16,192,128]{2,1,0:T(8,128)(2,1)}, bf16[18,192,128]{2,1,0:T(8,128)(2,1)}) custom-call(s32[5,4]{1,0:T(8,128)} %add_add_fusion.flags, bf16[3,16,192,128]{3,2,1,0:T(8,128)(2,1)} %all-gather.5.cloned.1.call-done.caches.frames, bf16[18,192,128]{2,1,0:T(8,128)(2,1)} %broadcast_in_dim.8.a_p.a_pp, ...), custom_call_target="tpu_custom_call" | custom-call | tf_op jit(solution)/shard_map/pallas_call | solution.py:282
  55.6 13.9 %all-gather.9.cloned.1.call-done = bf16[1,2,16,192,128]{4,3,2,1,0:T(8,128)(2,1)} async-done(((bf16[1,2,2,192,128]{4,3,2,1,0:T(8,128)(2,1)}), bf16[1,2,16,192,128]{4,3,2,1,0:T(8,128)(2,1)}) %all-gather.9.cloned.1.call-update) | async-done | bytes 1572880 | tf_op jit(solution)/shard_map/all_gather | solution.py:338
  69.4 7.2 %shard_map.78 = (bf16[8,192,128]{2,1,0:T(8,128)(2,1)}, bf16[18,192,128]{2,1,0:T(8,128)(2,1)}) custom-call(s32[5,4]{1,0:T(8,128)} %add_add_fusion.flags, bf16[2,16,192,128]{3,2,1,0:T(8,128)(2,1)} %bitcast.111, bf16[18,192,128]{2,1,0:T(8,128)(2,1)} %broadcast_in_dim.8.a_p.a_pp, bf16[18,192,128]{2,1,0:T(8,128)(2,1)} %broadcast_in_dim.8.a_p.a_pp, ...), custom_call_target="tpu_custom_call" | custom-call | tf_op jit(solution)/shard_map/pallas_call | solution.py:282
  76.6 3.6 %collective-permute-start = (bf16[8,192,128]{2,1,0:T(8,128)(2,1)}, bf16[8,192,128]{2,1,0:T(8,128)(2,1)S(1)}, u32[]{:S(2)}, u32[]{:S(2)}) collective-permute-start(bf16[8,192,128]{2,1,0:T(8,128)(2,1)} %get-tuple-element.32), channel_id=1, source_target_pairs={{0,8},{8,16},{16,24},{1,9},{9,17},{17,25},{2,10},{10,18},{18,26},{... | collective-permute-start | bytes 1179656 | tf_op jit(solution)/shard_map/ppermute | solution.py:384
  80.2 6.9 %shard_map.79 = bf16[8,192,128]{2,1,0:T(8,128)(2,1)} custom-call(s32[5,4]{1,0:T(8,128)} %add_add_fusion.flags, bf16[2,16,192,128]{3,2,1,0:T(8,128)(2,1)} %bitcast.112, bf16[18,192,128]{2,1,0:T(8,128)(2,1)} %broadcast_in_dim.8.a_p.a_pp, bf16[18,192,128]{2,1,0:T(8,128)(2,1)} %broadcast_in_dim.8.a_p.a_pp, ...), custom_call_target="tpu_custom_call" | custom-call | tf_op jit(solution)/shard_map/pallas_call | solution.py:282
  87.1 3.8 %collective-permute-done.src_b = bf16[8,192,128]{2,1,0:T(8,128)(2,1)S(1)} collective-permute-done((bf16[8,192,128]{2,1,0:T(8,128)(2,1)}, bf16[8,192,128]{2,1,0:T(8,128)(2,1)S(1)}, u32[]{:S(2)}, u32[]{:S(2)}) %collective-permute-start) | collective-permute-done | bytes 393248 | tf_op jit(solution)/shard_map/ppermute | solution.py:384
  90.9 4.8 %all-gather.7.cloned.1.call-done.frames = bf16[2,16,192,128]{3,2,1,0:T(8,128)(2,1)} async-done(((bf16[2,2,192,128]{3,2,1,0:T(8,128)(2,1)}), bf16[2,16,192,128]{3,2,1,0:T(8,128)(2,1)}) %all-gather.7.cloned.1.call-update) | async-done | bytes 1572880 | tf_op jit(solution)/shard_map/all_gather | solution.py:342
  96.4 10.2 %shard_map.80 = (bf16[16,192,128]{2,1,0:T(8,128)(2,1)}, bf16[18,192,128]{2,1,0:T(8,128)(2,1)}) custom-call(s32[5,4]{1,0:T(8,128)} %add_add_fusion.flags, bf16[3,16,192,128]{3,2,1,0:T(8,128)(2,1)} %all-gather.5.cloned.1.call-done.caches.frames, bf16[18,192,128]{2,1,0:T(8,128)(2,1)} %get-tuple-element.34.a_p.a_pp, ...), custom_call_target="tpu_custom_call" | custom-call | tf_op jit(solution)/shard_map/pallas_call | solution.py:282
  106.7 7.2 %shard_map.81 = (bf16[8,192,128]{2,1,0:T(8,128)(2,1)}, bf16[18,192,128]{2,1,0:T(8,128)(2,1)}) custom-call(s32[5,4]{1,0:T(8,128)} %add_add_fusion.flags, bf16[2,16,192,128]{3,2,1,0:T(8,128)(2,1)} %bitcast.113, bf16[18,192,128]{2,1,0:T(8,128)(2,1)} %get-tuple-element.31.rest_0_.a_p.a_pp, bf16[18,192,128]{2,1,0:T(8,128)(2,1)} %broadcast_in_dim.8.a_p.a_pp, ...), custom_call_target="tpu_custom_call" | custom-call | tf_op jit(solution)/shard_map/pallas_call | solution.py:282
  113.9 3.8 %collective-permute-start.2 = (bf16[8,192,128]{2,1,0:T(8,128)(2,1)}, bf16[8,192,128]{2,1,0:T(8,128)(2,1)S(1)}, u32[]{:S(2)}, u32[]{:S(2)}) collective-permute-start(bf16[8,192,128]{2,1,0:T(8,128)(2,1)} %get-tuple-element.37), channel_id=1, source_target_pairs={{0,8},{8,16},{16,24},{1,9},{9,17},{17,25},{2,10},{10,18},{18,26},{... | collective-permute-start | bytes 1179656 | tf_op jit(solution)/shard_map/ppermute | solution.py:384
  117.6 6.9 %shard_map.82 = bf16[8,192,128]{2,1,0:T(8,128)(2,1)} custom-call(s32[5,4]{1,0:T(8,128)} %add_add_fusion.flags, bf16[2,16,192,128]{3,2,1,0:T(8,128)(2,1)} %bitcast.114, bf16[18,192,128]{2,1,0:T(8,128)(2,1)} %get-tuple-element.31.rest_0_.a_p.a_pp, bf16[18,192,128]{2,1,0:T(8,128)(2,1)} %broadcast_in_dim.8.a_p.a_pp, ...), custom_call_target="tpu_custom_call" | custom-call | tf_op jit(solution)/shard_map/pallas_call | solution.py:282
  124.5 3.6 %collective-permute-done.2.src_b = bf16[8,192,128]{2,1,0:T(8,128)(2,1)S(1)} collective-permute-done((bf16[8,192,128]{2,1,0:T(8,128)(2,1)}, bf16[8,192,128]{2,1,0:T(8,128)(2,1)S(1)}, u32[]{:S(2)}, u32[]{:S(2)}) %collective-permute-start.2) | collective-permute-done | bytes 393248 | tf_op jit(solution)/shard_map/ppermute | solution.py:384
  128.1 1.7 collective-permute-done.3.src_c
  130.6 10.2 %shard_map.83 = (bf16[16,192,128]{2,1,0:T(8,128)(2,1)}, bf16[18,192,128]{2,1,0:T(8,128)(2,1)}) custom-call(s32[5,4]{1,0:T(8,128)} %add_add_fusion.flags, bf16[3,16,192,128]{3,2,1,0:T(8,128)(2,1)} %all-gather.5.cloned.1.call-done.caches.frames, bf16[18,192,128]{2,1,0:T(8,128)(2,1)} %get-tuple-element.39.a_p.a_pp, ...), custom_call_target="tpu_custom_call" | custom-call | tf_op jit(solution)/shard_map/pallas_call | solution.py:282
  140.8 7.2 %shard_map.84 = (bf16[8,192,128]{2,1,0:T(8,128)(2,1)}, bf16[18,192,128]{2,1,0:T(8,128)(2,1)}) custom-call(s32[5,4]{1,0:T(8,128)} %add_add_fusion.flags, bf16[2,16,192,128]{3,2,1,0:T(8,128)(2,1)} %bitcast.115, bf16[18,192,128]{2,1,0:T(8,128)(2,1)} %get-tuple-element.36.rest_0_.a_p.a_pp, bf16[18,192,128]{2,1,0:T(8,128)(2,1)} %get-tuple-element.31.rest_0_.a_p.a_pp, ...), custom_call_target="tpu_custom_call" | custom-call | tf_op jit(solution)/shard_map/pallas_call | solution.py:282
  148.0 2.6 %collective-permute-start.4 = (bf16[8,192,128]{2,1,0:T(8,128)(2,1)}, bf16[8,192,128]{2,1,0:T(8,128)(2,1)S(1)}, u32[]{:S(2)}, u32[]{:S(2)}) collective-permute-start(bf16[8,192,128]{2,1,0:T(8,128)(2,1)} %get-tuple-element.42), channel_id=1, source_target_pairs={{0,8},{8,16},{16,24},{1,9},{9,17},{17,25},{2,10},{10,18},{18,26},{... | collective-permute-start | bytes 1179656 | tf_op jit(solution)/shard_map/ppermute | solution.py:384
  150.7 6.8 %shard_map.85 = bf16[8,192,128]{2,1,0:T(8,128)(2,1)} custom-call(s32[5,4]{1,0:T(8,128)} %add_add_fusion.flags, bf16[2,16,192,128]{3,2,1,0:T(8,128)(2,1)} %bitcast.116, bf16[18,192,128]{2,1,0:T(8,128)(2,1)} %get-tuple-element.36.rest_0_.a_p.a_pp, bf16[18,192,128]{2,1,0:T(8,128)(2,1)} %get-tuple-element.31.rest_0_.a_p.a_pp, ...), custom_call_target="tpu_custom_call" | custom-call | tf_op jit(solution)/shard_map/pallas_call | solution.py:282
  157.5 4.7 %collective-permute-done.4.src_b = bf16[8,192,128]{2,1,0:T(8,128)(2,1)S(1)} collective-permute-done((bf16[8,192,128]{2,1,0:T(8,128)(2,1)}, bf16[8,192,128]{2,1,0:T(8,128)(2,1)S(1)}, u32[]{:S(2)}, u32[]{:S(2)}) %collective-permute-start.4) | collective-permute-done | bytes 393248 | tf_op jit(solution)/shard_map/ppermute | solution.py:384
  162.2 1.7 collective-permute-done.5.src_c
  164.7 10.3 %shard_map.86 = (bf16[16,192,128]{2,1,0:T(8,128)(2,1)}, bf16[18,192,128]{2,1,0:T(8,128)(2,1)}) custom-call(s32[5,4]{1,0:T(8,128)} %add_add_fusion.flags, bf16[3,16,192,128]{3,2,1,0:T(8,128)(2,1)} %all-gather.5.cloned.1.call-done.caches.frames, bf16[18,192,128]{2,1,0:T(8,128)(2,1)} %get-tuple-element.44.a_p.a_pp, ...), custom_call_target="tpu_custom_call" | custom-call | tf_op jit(solution)/shard_map/pallas_call | solution.py:282
  174.9 7.2 %shard_map.87 = (bf16[8,192,128]{2,1,0:T(8,128)(2,1)}, bf16[18,192,128]{2,1,0:T(8,128)(2,1)}) custom-call(s32[5,4]{1,0:T(8,128)} %add_add_fusion.flags, bf16[2,16,192,128]{3,2,1,0:T(8,128)(2,1)} %bitcast.117, bf16[18,192,128]{2,1,0:T(8,128)(2,1)} %get-tuple-element.41.rest_0_.a_p.a_pp, bf16[18,192,128]{2,1,0:T(8,128)(2,1)} %get-tuple-element.36.rest_0_.a_p.a_pp, ...), custom_call_target="tpu_custom_call" | custom-call | tf_op jit(solution)/shard_map/pallas_call | solution.py:282
  182.1 2.1 collective-permute-start.6
  184.2 6.9 %shard_map.88 = bf16[8,192,128]{2,1,0:T(8,128)(2,1)} custom-call(s32[5,4]{1,0:T(8,128)} %add_add_fusion.flags, bf16[2,16,192,128]{3,2,1,0:T(8,128)(2,1)} %bitcast.118, bf16[18,192,128]{2,1,0:T(8,128)(2,1)} %get-tuple-element.41.rest_0_.a_p.a_pp, bf16[18,192,128]{2,1,0:T(8,128)(2,1)} %get-tuple-element.36.rest_0_.a_p.a_pp, ...), custom_call_target="tpu_custom_call" | custom-call | tf_op jit(solution)/shard_map/pallas_call | solution.py:282
  191.2 5.1 %collective-permute-done.6.src_b = bf16[8,192,128]{2,1,0:T(8,128)(2,1)S(1)} collective-permute-done((bf16[8,192,128]{2,1,0:T(8,128)(2,1)}, bf16[8,192,128]{2,1,0:T(8,128)(2,1)S(1)}, u32[]{:S(2)}, u32[]{:S(2)}) %collective-permute-start.6) | collective-permute-done | bytes 393248 | tf_op jit(solution)/shard_map/ppermute | solution.py:384
  196.3 1.0 slice.52
  197.3 1.2 select_bitcast_fusion.3
  199.3 10.3 %shard_map.89 = (bf16[16,192,128]{2,1,0:T(8,128)(2,1)}, bf16[18,192,128]{2,1,0:T(8,128)(2,1)}) custom-call(s32[5,4]{1,0:T(8,128)} %add_add_fusion.flags, bf16[3,16,192,128]{3,2,1,0:T(8,128)(2,1)} %all-gather.5.cloned.1.call-done.caches.frames, bf16[18,192,128]{2,1,0:T(8,128)(2,1)} %get-tuple-element.53.a_p, ...), custom_call_target="tpu_custom_call" | custom-call | tf_op jit(solution)/shard_map/pallas_call | solution.py:282
  209.6 1.1 fusion.7
  210.8 9.5 %shard_map.90 = (bf16[16,192,128]{2,1,0:T(8,128)(2,1)}, bf16[18,192,128]{2,1,0:T(8,128)(2,1)}) custom-call(s32[5,4]{1,0:T(8,128)} %add_add_fusion.flags, bf16[2,16,192,128]{3,2,1,0:T(8,128)(2,1)} %bitcast.119, bf16[18,192,128]{2,1,0:T(8,128)(2,1)} %get-tuple-element.47.rest_0_.a_p, bf16[18,192,128]{2,1,0:T(8,128)(2,1)} %get-tuple-element.41.rest_0_.a_p.a_pp, ...), custom_call_target="tpu_custom_call" | custom-call | tf_op jit(solution)/shard_map/pallas_call | solution.py:282
  220.2 1.2 fusion.1
  221.5 1.2 copy.61
  222.7 1.2 select_bitcast_fusion.2
  223.9 0.9 copy.60
  (61 shorter events, 9.1 us)
Async XLA Ops:
  7.2 35.9 %all-gather.5.cloned.1.call-start = ((), (), s32[]{:S(2)}) async-start(), calls=%async_computation | async-start | bytes 2654208 | tf_op jit(solution)/shard_map/all_gather | solution.py:337
  10.0 59.4 %all-gather.9.cloned.1.call-start = ((), (), s32[]{:S(2)}) async-start(), calls=%async_computation.2 | async-start | bytes 1769472 | tf_op jit(solution)/shard_map/all_gather | solution.py:338
  10.8 84.9 %all-gather.7.cloned.1.call-start = ((), (), s32[]{:S(2)}) async-start(), calls=%async_computation.1 | async-start | bytes 1769472 | tf_op jit(solution)/shard_map/all_gather | solution.py:342
  19.8 4.4 %copy-start.10 = (f32[1,2,192]{2,1,0:T(2,128)S(1)}, f32[1,2,192]{2,1,0:T(2,128)}, u32[]{:S(2)}) copy-start(f32[1,2,192]{2,1,0:T(2,128)} %param.9) | copy-start | bytes 4612
  19.8 5.2 %copy-start.11 = (f32[1,2,192]{2,1,0:T(2,128)S(1)}, f32[1,2,192]{2,1,0:T(2,128)}, u32[]{:S(2)}) copy-start(f32[1,2,192]{2,1,0:T(2,128)} %param.10) | copy-start | bytes 4612
  19.8 6.0 %copy-start.12 = (f32[1,2,192]{2,1,0:T(2,128)S(1)}, f32[1,2,192]{2,1,0:T(2,128)}, u32[]{:S(2)}) copy-start(f32[1,2,192]{2,1,0:T(2,128)} %param.11) | copy-start | bytes 4612
  30.6 6.6 %copy-start.13 = (s32[4]{0:T(128)S(1)}, s32[4]{0:T(128)}, u32[]{:S(2)}) copy-start(s32[4]{0:T(128)} %pad.15.clone) | copy-start | bytes 52
  76.6 14.3 %collective-permute-start = (bf16[8,192,128]{2,1,0:T(8,128)(2,1)}, bf16[8,192,128]{2,1,0:T(8,128)(2,1)S(1)}, u32[]{:S(2)}, u32[]{:S(2)}) collective-permute-start(bf16[8,192,128]{2,1,0:T(8,128)(2,1)} %get-tuple-element.32), channel_id=1, source_target_pairs={{0,8},{8,16},{16,24},{1,9},{9,17},{17,25},{2,10},{10,18},{18,26},{... | collective-permute-start | bytes 1179656 | tf_op jit(solution)/shard_map/ppermute | solution.py:384
  90.9 4.8 %copy-start.1 = (bf16[8,192,128]{2,1,0:T(8,128)(2,1)}, bf16[8,192,128]{2,1,0:T(8,128)(2,1)S(1)}, u32[]{:S(2)}) copy-start(bf16[8,192,128]{2,1,0:T(8,128)(2,1)S(1)} %collective-permute-done.src_b) | copy-start | bytes 1179652
  90.9 4.8 %collective-permute-start.1 = (bf16[8,192,128]{2,1,0:T(8,128)(2,1)S(1)}, bf16[8,192,128]{2,1,0:T(8,128)(2,1)S(1)}, u32[]{:S(2)}, u32[]{:S(2)}) collective-permute-start(bf16[8,192,128]{2,1,0:T(8,128)(2,1)S(1)} %collective-permute-done.src_b), channel_id=1, source_target_pairs={{0,1},{1,0},{2,3},{3,2},{4,5},{5,4},{6,7},{7,6},{8,9},{9,8},{10,11... | collective-permute-start | bytes 1179656 | tf_op jit(solution)/shard_map/ppermute | solution.py:386
  95.7 0.8 copy-start.4
  113.9 14.3 %collective-permute-start.2 = (bf16[8,192,128]{2,1,0:T(8,128)(2,1)}, bf16[8,192,128]{2,1,0:T(8,128)(2,1)S(1)}, u32[]{:S(2)}, u32[]{:S(2)}) collective-permute-start(bf16[8,192,128]{2,1,0:T(8,128)(2,1)} %get-tuple-element.37), channel_id=1, source_target_pairs={{0,8},{8,16},{16,24},{1,9},{9,17},{17,25},{2,10},{10,18},{18,26},{... | collective-permute-start | bytes 1179656 | tf_op jit(solution)/shard_map/ppermute | solution.py:384
  128.1 1.7 copy-start.2
  128.1 1.7 collective-permute-start.3
  129.8 0.7 copy-start.5
  148.0 14.2 %collective-permute-start.4 = (bf16[8,192,128]{2,1,0:T(8,128)(2,1)}, bf16[8,192,128]{2,1,0:T(8,128)(2,1)S(1)}, u32[]{:S(2)}, u32[]{:S(2)}) collective-permute-start(bf16[8,192,128]{2,1,0:T(8,128)(2,1)} %get-tuple-element.42), channel_id=1, source_target_pairs={{0,8},{8,16},{16,24},{1,9},{9,17},{17,25},{2,10},{10,18},{18,26},{... | collective-permute-start | bytes 1179656 | tf_op jit(solution)/shard_map/ppermute | solution.py:384
  162.2 1.7 copy-start.3
  162.2 1.7 collective-permute-start.5
  163.9 0.7 copy-start.6
  182.1 14.2 %collective-permute-start.6 = (bf16[8,192,128]{2,1,0:T(8,128)(2,1)}, bf16[8,192,128]{2,1,0:T(8,128)(2,1)S(1)}, u32[]{:S(2)}, u32[]{:S(2)}) collective-permute-start(bf16[8,192,128]{2,1,0:T(8,128)(2,1)} %get-tuple-element.46), channel_id=1, source_target_pairs={{0,8},{8,16},{16,24},{1,9},{9,17},{17,25},{2,10},{10,18},{18,26},{... | collective-permute-start | bytes 1179656 | tf_op jit(solution)/shard_map/ppermute | solution.py:384
  184.2 12.0 %copy-start = (bf16[1,2,16,192,128]{4,3,2,1,0:T(8,128)(2,1)S(1)}, bf16[1,2,16,192,128]{4,3,2,1,0:T(8,128)(2,1)}, u32[]{:S(2)}) copy-start(bf16[1,2,16,192,128]{4,3,2,1,0:T(8,128)(2,1)} %all-gather.9.cloned.1.call-done) | copy-start | bytes 4718596
  191.2 6.1 %copy-start.9 = (bf16[8,192,128]{2,1,0:T(8,128)(2,1)S(1)}, bf16[8,192,128]{2,1,0:T(8,128)(2,1)}, u32[]{:S(2)}) copy-start(bf16[8,192,128]{2,1,0:T(8,128)(2,1)} %shard_map.82) | copy-start | bytes 1179652
  196.3 2.3 copy-start.7
  196.3 2.2 collective-permute-start.7
  198.5 0.8 copy-start.8
  199.3 10.3 %slice-start = ((bf16[3,16,192,128]{3,2,1,0:T(8,128)(2,1)}), bf16[1,16,192,128]{3,2,1,0:T(8,128)(2,1)S(1)}, s32[]{:S(2)}) async-start(bf16[3,16,192,128]{3,2,1,0:T(8,128)(2,1)} %all-gather.5.cloned.1.call-done.caches.frames), calls=%async_computation.3 | async-start | bytes 1572864 | tf_op jit(solution)/shard_map/slice | solution.py:390
Sparse Core Ops, SparseCore 0:
  10.2 32.8 all-gather.4
  45.2 24.1 all-gather.8
  71.0 24.5 all-gather.6
